TPU v7x, 128 devices: a whole 4x4x4 slice. The times are simulated.
128 devices in a mesh: seq: 32 (over x, y_lo, z), tp: 2 (over core), pd: 2 (over y_hi).
Axes of the slice: x: 4, y: 4 (y_hi: 2, y_lo: 2; y = y_hi * 2 + y_lo), z: 4, core: 2. Of those that a mesh axis runs over, the one named last changes fastest.
Arguments:
- hidden_in: bfloat16 [2, 8192, 2048], P('pd', 'seq'), may hold values from -6 to 6
- input_gain: float32 [2048], replicated, may hold values from 0.5 to 1.5
- w_query: bfloat16 [2048, 2048], P(None, 'tp'), may hold values from -0.125 to 0.125
- w_key: bfloat16 [2048, 256], P(None, 'tp'), may hold values from -0.125 to 0.125
- w_value: bfloat16 [2048, 256], P(None, 'tp'), may hold values from -0.125 to 0.125
- q_gain: float32 [128], replicated, may hold values from 0.1 to 1.9
- k_gain: float32 [128], replicated, may hold values from 0.1 to 1.9
- w_out: bfloat16 [2048, 2048], P('tp'), may hold values from -0.125 to 0.125
- post_gain: float32 [2048], replicated, may hold values from 0.5 to 1.5
- ctx_key: bfloat16 [2, 2048, 256], P('pd', 'seq', 'tp'), may hold values from -70 to 70
- ctx_value: bfloat16 [2, 2048, 256], P('pd', 'seq', 'tp'), may hold values from -6 to 6
- span_lens: int32 [2, 8], P('pd'), may hold values from 1 to 4096, 8192 in all within a row
- ctx_lens: int32 [2, 8], P('pd'), may hold values from 1 to 1024, 2048 in all within a row
- route_ids: int32 [2, 8192, 8], P('pd', ('seq', 'tp')), may hold values from 0 to 127, all different within a row; in each aligned block of 128 rows (0 to 127, 128 to 255, ..., all dimensions but the last counted through in order) at most 12 rows name the same one
- route_weights: float32 [2, 8192, 8], P('pd', ('seq', 'tp')), may hold values from 0.05 to 1
- w_gate_up: bfloat16 [128, 2048, 1536], P(('seq', 'tp', 'pd')), may hold values from -0.125 to 0.125
- w_down: bfloat16 [128, 768, 2048], P(('seq', 'tp', 'pd')), may hold values from -0.21875 to 0.21875
- earlier_kv: bfloat16 [8, 2, 8192, 2, 256], P(None, 'pd', 'seq', 'tp'), may hold values from -6 to 6
- page_table: int32 [8, 2, 64, 2], P(None, 'pd', 'seq', 'tp'), may hold values from 0 to 511, as said below
Outputs:
- layer_out: bfloat16 [2, 8192, 2048], P('pd', ('seq', 'tp'))
- decode_cache: bfloat16 [32, 2, 2, 16, 128, 256], P('seq', 'tp', 'pd')
Inputs may be any that keep to these rules, and one draw needn't show every extreme that they name: `route_ids`: within the rows of one device no expert is named more than 12 times, a bound that some block reaches. `page_table`: an entry owner * 16 + slot sends the page to that slot of the device at index owner of seq, with the same indices of tp and pd. Every slot of every owner receives exactly one page; one device sends at most 1 pages to one owner, and exactly that many to some owner.
All inputs are finite; a program needn't handle non-finite values.
Results may differ from a plain program's by a relative error of at most 0.015.
Values may be sent and summed in bfloat16 or wider, within the bound.
No kernel may reach another device: no remote copies, remote signals or barrier semaphores. Data moves between devices by JAX's collectives and lax.ppermute only.
A program may use at most 128 MiB of HBM per device.

v0:
```python
import functools
import math

import jax
import jax.numpy as jnp
from jax import lax
from jax.experimental import pallas as pl
from jax.experimental.pallas import tpu as pltpu
from jax.sharding import PartitionSpec as P

PAGE = 128


def rms_norm(values, gain):
    return values * lax.rsqrt(jnp.mean(values * values, axis=-1, keepdims=True) + 1e-06) * gain


def rotate(values, places):
    half = values.shape[-1] // 2
    freq = jnp.exp(
        jnp.arange(half, dtype=jnp.float32) * (-2.0 * math.log(1000000.0) / values.shape[-1])
    )
    angle = places.astype(jnp.float32)[:, None] * freq[None, :]
    cosine = jnp.cos(angle)[:, None, :]
    sine = jnp.sin(angle)[:, None, :]
    first = values[..., :half]
    second = values[..., half:]
    return jnp.concatenate(
        [first * cosine - second * sine, second * cosine + first * sine], axis=-1
    )


def query_places(lengths, context_lengths, places):
    ends = jnp.cumsum(lengths)
    starts = ends - lengths
    request = jnp.sum((places[:, None] >= ends[None, :]).astype(jnp.int32), axis=1)
    member = request[:, None] == jnp.arange(lengths.shape[0], dtype=jnp.int32)[None, :]
    first = jnp.sum(jnp.where(member, starts[None, :], 0), axis=1)
    prior = jnp.sum(jnp.where(member, context_lengths[None, :], 0), axis=1)
    return (request, places - first + prior)


def context_places(context_lengths, places):
    ends = jnp.cumsum(context_lengths)
    starts = ends - context_lengths
    request = jnp.sum((places[:, None] >= ends[None, :]).astype(jnp.int32), axis=1)
    member = request[:, None] == jnp.arange(context_lengths.shape[0], dtype=jnp.int32)[None, :]
    first = jnp.sum(jnp.where(member, starts[None, :], 0), axis=1)
    return (request, places - first)


KEY_BLOCK = 512


def flash_kernel(nkb, scale, live_ref, qreq_ref, qpos_ref, kreq_ref, kpos_ref, q_ref, k_ref, v_ref, o_ref, m_sc, l_sc, acc_sc):
    kb = pl.program_id(0)

    @pl.when(kb == 0)
    def _():
        m_sc[...] = jnp.full(m_sc.shape, -1e30, jnp.float32)
        l_sc[...] = jnp.zeros(l_sc.shape, jnp.float32)
        acc_sc[...] = jnp.zeros(acc_sc.shape, jnp.float32)

    @pl.when(live_ref[kb] > 0)
    def _():
        scores = lax.dot_general(
            q_ref[...], k_ref[...], (((1,), (1,)), ((), ())), preferred_element_type=jnp.float32
        ) * scale
        visible = (qreq_ref[...] == kreq_ref[...]) & (kpos_ref[...] <= qpos_ref[...])
        heads = scores.shape[0] // visible.shape[0]
        scores = jnp.where(
            visible[None], scores.reshape((heads,) + visible.shape), -jnp.inf
        ).reshape(scores.shape)
        m_old = m_sc[...]
        m_new = jnp.maximum(m_old, jnp.max(scores, axis=1, keepdims=True))
        expo = jnp.exp(scores - m_new)
        factor = jnp.exp(m_old - m_new)
        l_sc[...] = factor * l_sc[...] + jnp.sum(expo, axis=1, keepdims=True)
        acc_sc[...] = factor * acc_sc[...] + jnp.dot(
            expo.astype(jnp.bfloat16), v_ref[...], preferred_element_type=jnp.float32
        )
        m_sc[...] = m_new

    @pl.when(kb == nkb - 1)
    def _():
        o_ref[...] = (acc_sc[...] / l_sc[...]).astype(o_ref.dtype)


def flash_attention(live, qreq, qpos, kreq, kpos, q, k, v, scale):
    rows, head_dim = q.shape
    length = k.shape[0]
    nkb = length // KEY_BLOCK
    grid_spec = pltpu.PrefetchScalarGridSpec(
        num_scalar_prefetch=1,
        grid=(nkb,),
        in_specs=[
            pl.BlockSpec(qreq.shape, lambda kb, live: (0, 0)),
            pl.BlockSpec(qpos.shape, lambda kb, live: (0, 0)),
            pl.BlockSpec((1, KEY_BLOCK), lambda kb, live: (0, kb)),
            pl.BlockSpec((1, KEY_BLOCK), lambda kb, live: (0, kb)),
            pl.BlockSpec((rows, head_dim), lambda kb, live: (0, 0)),
            pl.BlockSpec((KEY_BLOCK, head_dim), lambda kb, live: (kb, 0)),
            pl.BlockSpec((KEY_BLOCK, head_dim), lambda kb, live: (kb, 0)),
        ],
        out_specs=pl.BlockSpec((rows, head_dim), lambda kb, live: (0, 0)),
        scratch_shapes=[
            pltpu.VMEM((rows, 1), jnp.float32),
            pltpu.VMEM((rows, 1), jnp.float32),
            pltpu.VMEM((rows, head_dim), jnp.float32),
        ],
    )
    flops = 4 * rows * length * head_dim
    return pl.pallas_call(
        functools.partial(flash_kernel, nkb, scale),
        grid_spec=grid_spec,
        out_shape=jax.ShapeDtypeStruct((rows, head_dim), jnp.bfloat16),
        compiler_params=pltpu.CompilerParams(dimension_semantics=("arbitrary",)),
        cost_estimate=pl.CostEstimate(
            flops=flops, transcendentals=rows * length, bytes_accessed=2 * length * head_dim * 2 + 2 * rows * head_dim * 2
        ),
    )(live, qreq, qpos, kreq, kpos, q, k, v)


def expert_mlp(arrived, w_gate_up, w_down):
    hidden = jnp.einsum("sejd,edf->sejf", arrived, w_gate_up, preferred_element_type=jnp.float32)
    inner = hidden.shape[-1] // 2
    act = (jax.nn.silu(hidden[..., :inner]) * hidden[..., inner:]).astype(jnp.bfloat16)
    return jnp.einsum("sejf,efd->sejd", act, w_down, preferred_element_type=jnp.float32).astype(
        jnp.bfloat16
    )


def shards(
    hidden_in,
    input_gain,
    w_query,
    w_key,
    w_value,
    q_gain,
    k_gain,
    w_out,
    post_gain,
    ctx_key,
    ctx_value,
    span_lens,
    ctx_lens,
    route_ids,
    route_weights,
    w_gate_up,
    w_down,
    earlier_kv,
    page_table,
):
    tokens = hidden_in[0]
    tok_count = tokens.shape[0]
    width = tokens.shape[1]
    ctx_count = ctx_key.shape[1]
    head_dim = q_gain.shape[0]
    seq_index = lax.axis_index("seq")
    span_places = seq_index * tok_count + jnp.arange(tok_count, dtype=jnp.int32)
    ctx_index = seq_index * ctx_count + jnp.arange(ctx_count, dtype=jnp.int32)
    query_req, query_pos = query_places(span_lens[0], ctx_lens[0], span_places)
    ctx_req, ctx_pos = context_places(ctx_lens[0], ctx_index)
    normed = rms_norm(tokens.astype(jnp.float32), input_gain).astype(jnp.bfloat16)
    query = jnp.dot(normed, w_query, preferred_element_type=jnp.float32)
    key_proj = jnp.dot(normed, w_key, preferred_element_type=jnp.float32)
    value_proj = jnp.dot(normed, w_value, preferred_element_type=jnp.float32).astype(jnp.bfloat16)
    query_heads = w_query.shape[1] // head_dim
    kv_local = w_key.shape[1] // head_dim
    group = query_heads // kv_local
    queries = rotate(
        rms_norm(query.reshape(tok_count, query_heads, head_dim), q_gain), query_pos
    ).astype(jnp.bfloat16)
    queries = queries.reshape(tok_count, kv_local, group, head_dim).transpose(1, 2, 0, 3)
    span_keys = rotate(
        rms_norm(key_proj.reshape(tok_count, kv_local, head_dim), k_gain), query_pos
    ).astype(jnp.bfloat16)
    all_keys = jnp.concatenate(
        [ctx_key[0], span_keys.reshape(tok_count, kv_local * head_dim)], axis=0
    )
    all_values = jnp.concatenate([ctx_value[0], value_proj], axis=0)
    seq_size = lax.axis_size("seq")
    every_ctx_req, every_ctx_pos = context_places(
        ctx_lens[0], jnp.arange(seq_size * ctx_count, dtype=jnp.int32)
    )
    every_query_req, every_query_pos = query_places(
        span_lens[0], ctx_lens[0], jnp.arange(seq_size * tok_count, dtype=jnp.int32)
    )
    key_req = jnp.concatenate([every_ctx_req, every_query_req], axis=0)
    key_pos = jnp.concatenate([every_ctx_pos, every_query_pos], axis=0)
    scale = 1.0 / math.sqrt(head_dim)
    kv_width = kv_local * head_dim
    local_kv = jnp.concatenate([all_keys, all_values], axis=1)
    every_kv = lax.all_to_all(
        jnp.broadcast_to(local_kv[None], (seq_size,) + local_kv.shape),
        "seq",
        split_axis=0,
        concat_axis=0,
        tiled=True,
    )
    layers = earlier_kv.shape[0]
    per_device = tok_count // PAGE
    page_count = layers * per_device
    page_cap = max(1, page_count // seq_size)
    pages = earlier_kv[:, 0].reshape(layers, per_device, PAGE, kv_local, 2 * head_dim)
    pages = pages.transpose(3, 0, 1, 2, 4).reshape(kv_local, page_count, PAGE, 2 * head_dim)
    table = page_table[:, 0].transpose(2, 0, 1).reshape(kv_local, page_count)
    owners = table // page_count
    slots = table % page_count
    order = jnp.arange(page_count, dtype=jnp.int32)
    same = (owners[:, :, None] == owners[:, None, :]) & (
        order[None, None, :] < order[None, :, None]
    )
    page_rank = jnp.sum(same.astype(jnp.int32), axis=2)
    page_target = owners * page_cap + page_rank
    head_rows = jnp.broadcast_to(jnp.arange(kv_local, dtype=jnp.int32)[:, None], page_target.shape)
    outgoing_pages = (
        jnp.zeros((kv_local, seq_size * page_cap, PAGE, 2 * head_dim), jnp.bfloat16)
        .at[head_rows, page_target]
        .set(pages)
    )
    outgoing_slots = (
        jnp.full((kv_local, seq_size * page_cap), -1, jnp.int32)
        .at[head_rows, page_target]
        .set(slots)
    )
    slot_rows = 16
    slot_block = jnp.broadcast_to(
        outgoing_slots.astype(jnp.bfloat16)[:, :, None, None],
        (kv_local, seq_size * page_cap, slot_rows, 2 * head_dim),
    )
    outgoing_pages = jnp.concatenate([outgoing_pages, slot_block], axis=2)
    outgoing_pages, every_kv = lax.optimization_barrier((outgoing_pages, every_kv))
    arrived_both = lax.all_to_all(outgoing_pages, "seq", split_axis=1, concat_axis=1, tiled=True)
    arrived_pages = arrived_both[:, :, :PAGE]
    arrived_slots = arrived_both[:, :, PAGE, 0].astype(jnp.int32)
    ordered_kv = jnp.concatenate(
        [every_kv[:, :ctx_count].reshape(-1, 2 * kv_width), every_kv[:, ctx_count:].reshape(-1, 2 * kv_width)],
        axis=0,
    )
    length = ordered_kv.shape[0]
    seen = (query_req[:, None] == key_req[None, :]) & (key_pos[None, :] <= query_pos[:, None])
    live = jnp.any(jnp.any(seen, axis=0).reshape(length // KEY_BLOCK, KEY_BLOCK), axis=1).astype(jnp.int32)
    rows = group * tok_count
    qreq_rows = query_req.reshape(tok_count, 1)
    qpos_rows = query_pos.reshape(tok_count, 1)
    heads_out = []
    for h in range(kv_local):
        heads_out.append(
            flash_attention(
                live,
                qreq_rows,
                qpos_rows,
                key_req.reshape(1, length),
                key_pos.reshape(1, length),
                queries[h].reshape(rows, head_dim),
                ordered_kv[:, h * head_dim:(h + 1) * head_dim],
                ordered_kv[:, kv_width + h * head_dim:kv_width + (h + 1) * head_dim],
                scale,
            ).reshape(group, tok_count, head_dim)
        )
    attn = (
        jnp.stack(heads_out, axis=0)
        .transpose(2, 0, 1, 3)
        .reshape(tok_count, query_heads * head_dim)
    )
    half = tok_count // lax.axis_size("tp")
    proj = lax.psum_scatter(
        jnp.dot(attn, w_out, preferred_element_type=jnp.float32).astype(jnp.bfloat16),
        "tp",
        scatter_dimension=0,
        tiled=True,
    ).astype(jnp.float32)
    own_rows = lax.dynamic_slice_in_dim(tokens, lax.axis_index("tp") * half, half, 0)
    resid = (own_rows.astype(jnp.float32) + proj).astype(jnp.bfloat16)
    mixed = rms_norm(resid.astype(jnp.float32), post_gain).astype(jnp.bfloat16)
    top = route_ids.shape[2]
    row_ids = route_ids[0].reshape(-1)
    row_count = row_ids.shape[0]
    seq_tp = lax.axis_size("seq") * lax.axis_size("tp")
    pd_count = lax.axis_size("pd")
    device_count = seq_tp * pd_count
    exp_local = w_gate_up.shape[0]
    experts = device_count * exp_local
    capacity = max(2, 3 * tok_count * top // (2 * lax.axis_size("tp") * experts))
    picks = (row_ids[:, None] == jnp.arange(experts, dtype=jnp.int32)[None, :]).astype(jnp.bfloat16)
    earlier = (
        lax.broadcasted_iota(jnp.int32, (row_count, row_count), 0)
        > lax.broadcasted_iota(jnp.int32, (row_count, row_count), 1)
    ).astype(jnp.bfloat16)
    before = jnp.dot(earlier, picks, preferred_element_type=jnp.float32)
    rank = jnp.sum(before * picks.astype(jnp.float32), axis=1).astype(jnp.int32)
    target = row_ids * capacity + rank
    row_token = jnp.arange(row_count, dtype=jnp.int32) // top
    lanes = 128
    chunks = width // lanes
    moe_axes = ("seq", "tp", "pd")
    slot_of = (
        target.reshape(half, top)[None, :, :]
        == jnp.arange(experts * capacity, dtype=jnp.int32)[:, None, None]
    )
    placing_rows = jnp.any(slot_of, axis=2).astype(jnp.bfloat16)
    outgoing = jnp.dot(placing_rows, mixed, preferred_element_type=jnp.float32).astype(jnp.bfloat16)
    outgoing = outgoing.reshape(device_count, exp_local * capacity * chunks, lanes)
    outgoing, arrived_pages, arrived_slots = lax.optimization_barrier(
        (outgoing, arrived_pages, arrived_slots)
    )
    arrived = lax.all_to_all(outgoing, moe_axes, split_axis=0, concat_axis=0, tiled=True)
    done = expert_mlp(arrived.reshape(device_count, exp_local, capacity, width), w_gate_up, w_down)
    returned = lax.all_to_all(
        done.reshape(device_count, exp_local * capacity * chunks, lanes),
        moe_axes,
        split_axis=0,
        concat_axis=0,
        tiled=True,
    )
    gathered = returned.reshape(experts * capacity, chunks, lanes)[target]
    weights = route_weights[0]
    weights = weights / jnp.sum(weights, axis=-1, keepdims=True)
    moe = jnp.einsum(
        "tkcl,tk->tcl",
        gathered.reshape(half, top, chunks, lanes),
        weights,
        preferred_element_type=jnp.float32,
    ).reshape(half, width)
    layer_out = (resid.astype(jnp.float32) + moe).astype(jnp.bfloat16)[None]
    placing = (arrived_slots[:, None, :] == order[None, :, None]).astype(jnp.bfloat16)
    cache = jnp.einsum(
        "hkr,hrpc->hkpc", placing, arrived_pages, preferred_element_type=jnp.float32
    ).astype(jnp.bfloat16)
    decode_cache = cache[None, :, None]
    return (layer_out, decode_cache)


def solution(mesh):
    in_specs = (
        P("pd", "seq", None),
        P(),
        P(None, "tp"),
        P(None, "tp"),
        P(None, "tp"),
        P(),
        P(),
        P("tp", None),
        P(),
        P("pd", "seq", "tp"),
        P("pd", "seq", "tp"),
        P("pd", None),
        P("pd", None),
        P("pd", ("seq", "tp"), None),
        P("pd", ("seq", "tp"), None),
        P(("seq", "tp", "pd"), None, None),
        P(("seq", "tp", "pd"), None, None),
        P(None, "pd", "seq", "tp", None),
        P(None, "pd", "seq", "tp"),
    )
    out_specs = (P("pd", ("seq", "tp"), None), P("seq", "tp", "pd", None, None, None))
    return jax.shard_map(shards, mesh=mesh, in_specs=in_specs, out_specs=out_specs, check_vma=False)
```

profile of v0, /device:TPU:25, one launch (start us, length us, event | category | flops | bytes accessed | tf_op | source)
XLA Modules:
  0.0 442.6 jit_solution(2796559512405258195)
XLA Ops:
  7.2 1.0 reduce-window.6
  8.2 0.7 fusion.71
  8.9 1.5 fusion.16
  10.4 0.8 copy.128
  11.2 0.8 copy.129
  12.1 2.0 convolution_convert_fusion.2
  14.0 2.0 multiply_reduce_fusion.1
  16.9 2.9 broadcast_in_dim.151
  19.8 9.0 %all-to-all-start = ((bf16[32,320,256]{2,1,0:T(8,128)(2,1)}), bf16[32,320,256]{2,1,0:T(8,128)(2,1)}, u32[]{:S(2)}, u32[]{:S(2)}) async-start(bf16[32,320,256]{2,1,0:T(8,128)(2,1)} %broadcast_in_dim.151), calls=%async_computation | async-start | bytes 10485760 | tf_op jit(solution)/shard_map/all_to_all | solution.py:194
  30.9 3.0 and_reduce_fusion
  34.9 0.8 copy.132.qreq_ref
  35.7 7.0 %copy.149 = bf16[1024,2048]{1,0:T(8,128)(2,1)} copy(bf16[1024,2048]{0,1:T(8,128)(2,1)} %bitcast.169) | data formatting | bytes 8388608 | tf_op jit(solution)/shard_map/dot_general | solution.py:165
  42.8 3.9 multiply_reduce_fusion
  47.4 0.8 maximum_bitcast_fusion
  48.2 2.0 copy.124
  50.3 1.5 broadcast.440
  51.8 3.4 scatter_fusion
  55.3 3.2 pad_maximum_fusion.1
  58.5 0.7 subtract_add_fusion.qpos_ref
  59.2 34.6 %all-to-all-done = bf16[32,320,256]{2,1,0:T(8,128)(2,1)} async-done(((bf16[32,320,256]{2,1,0:T(8,128)(2,1)}), bf16[32,320,256]{2,1,0:T(8,128)(2,1)}, u32[]{:S(2)}, u32[]{:S(2)}) %all-to-all-start) | async-done | bytes 5242912 | tf_op jit(solution)/shard_map/all_to_all | solution.py:194
  93.7 1.3 slice.40
  95.0 2.5 slice.41
  97.5 5.4 %pad_maximum_fusion = (bf16[10240,128]{1,0:T(8,128)(2,1)}, bf16[10240,128]{1,0:T(8,128)(2,1)}) fusion(bf16[8192,256]{1,0:T(8,128)(2,1)S(1)} %bitcast.163, bf16[2048,256]{1,0:T(8,128)(2,1)S(1)} %bitcast.168), kind=kLoop, calls=%fused_computation.25 | loop fusion | flops 10485760 | bytes 10485760 | tf_op jit(solution)/shard_map/concatenate | solution.py:237
  102.9 26.8 %shard_map.194 = bf16[2048,128]{1,0:T(8,128)(2,1)} custom-call(s32[20]{0:T(128)} %convert_element_type.164.live_ref, s32[256,1]{1,0:T(8,128)} %copy.132.qreq_ref, s32[256,1]{1,0:T(8,128)} %subtract_add_fusion.qpos_ref, s32[1,10240]{1,0:T(1,128)} %bitcast.177, s32[1,10240]{1,0:T(1,128)} %bitcast.178, bf16[2048,128]{1,0:T(8,128)(2,1)} %bitcast.174, ...), custom_call_target="tpu_custom_call" | custom-call | flops 10737418240 | bytes 6291456 | tf_op jit(solution)/shard_map/pallas_call | solution.py:113
  129.7 2.0 copy.133
  131.7 4.6 %convolution_convert_fusion.1 = bf16[256,2048]{1,0:T(8,128)(2,1)} fusion(bf16[256,1024]{0,1:T(8,128)(2,1)} %bitcast.176, bf16[1024,2048]{1,0:T(8,128)(2,1)} %param.26), kind=kOutput, calls=%fused_computation.26 | convolution fusion | flops 1074266112 | bytes 5767168 | tf_op jit(solution)/shard_map/dot_general | solution.py:269
  136.4 31.7 %all-to-all-start.1 = ((bf16[1,32,144,256]{3,2,0,1:T(8,128)(2,1)}), bf16[1,32,144,256]{3,2,0,1:T(8,128)(2,1)}, u32[]{:S(2)}, u32[]{:S(2)}) async-start(bf16[1,32,144,256]{3,2,0,1:T(8,128)(2,1)} %bitcast.165), calls=%async_computation.2 | async-start | bytes 4718592 | tf_op jit(solution)/shard_map/all_to_all | solution.py:234
  169.1 5.6 %fusion.2 = pred[1536,128]{1,0:T(8,128)(4,1)S(1)} fusion(s32[128,8]{0,1:T(8,128)S(1)} %copy.136), kind=kLoop, calls=%fused_computation.9 | loop fusion | flops 2949120 | bytes 200704 | tf_op jit(solution)/shard_map/reduce_or | solution.py:302
  174.8 1.5 fusion.31
  176.3 0.8 copy-done.1
  177.0 4.5 %convolution_convert_fusion = bf16[1536,2048]{1,0:T(8,128)(2,1)} fusion(pred[1536,128]{1,0:T(8,128)(4,1)S(1)} %fusion.2, bf16[128,2048]{1,0:T(8,128)(2,1)S(1)} %get-tuple-element.29, f32[2048]{0:T(1024)S(1)} %copy-done.6, f32[128]{0:T(128)S(1)} %add_rsqrt_fusion.3), kind=kOutput, calls=%fused_computation.4 | convolution fusion | flops 809500672 | bytes 7021056 | tf_op jit(solution)/shard_map/dot_general | solution.py:303
  181.6 10.4 %reshape.739 = bf16[128,192,128]{2,1,0:T(8,128)(2,1)} reshape(bf16[1536,2048]{1,0:T(8,128)(2,1)} %convolution_convert_fusion) | data formatting | bytes 12582912 | tf_op jit(solution)/shard_map/reshape | solution.py:304
  192.0 3.4 all-to-all-done.1
  195.4 1.5 fusion.62
  196.9 3.2 slice.60
  200.1 86.7 %all_to_all.20 = bf16[128,192,128]{2,1,0:T(8,128)(2,1)} all-to-all(bf16[128,192,128]{2,1,0:T(8,128)(2,1)} %reshape.739), channel_id=1, replica_groups=mesh['seq'=32,'tp'=2,'pd'=2] {'seq','tp','pd'}, dimensions={0} | all-to-all | bytes 12582912 | tf_op jit(solution)/shard_map/all_to_all | solution.py:308
  286.7 9.2 %copy.138 = bf16[128,192,128]{0,2,1:T(8,128)(2,1)} copy(bf16[128,192,128]{2,1,0:T(8,128)(2,1)} %all_to_all.20) | data formatting | bytes 12582912 | tf_op jit(solution)/shard_map/all_to_all | solution.py:308
  296.0 14.5 %fusion.3 = f32[128,1,12,1536]{3,0,2,1:T(8,128)S(1)} fusion(bf16[128,12,2048]{0,2,1:T(8,128)(2,1)} %bitcast.167, bf16[1,2048,1536]{2,1,0:T(8,128)(2,1)} %param.34), kind=kOutput, calls=%fused_computation.10 | convolution fusion | flops 9663676416 | bytes 22020096 | tf_op jit(solution)/shard_map/sejd,edf->sejf/dot_general | solution.py:125
  310.5 7.1 %convert_bitcast_fusion = bf16[128,1,12,2048]{3,0,2,1:T(8,128)(2,1)} fusion(bf16[1,768,2048]{2,1,0:T(8,128)(2,1)S(1)} %copy-done, f32[128,1,12,1536]{3,0,2,1:T(8,128)S(1)} %fusion.3), kind=kOutput, calls=%fused_computation.7 | convolution fusion | flops 4842061824 | bytes 18874368 | tf_op jit(solution)/shard_map/sejf,efd->sejd/dot_general | solution.py:128
  317.5 8.7 %copy.140 = bf16[128,1,12,2048]{0,3,2,1:T(8,128)(2,1)} copy(bf16[128,1,12,2048]{3,0,2,1:T(8,128)(2,1)} %convert_bitcast_fusion) | data formatting | bytes 12582912 | tf_op jit(solution)/shard_map/convert_element_type | solution.py:128
  326.2 9.0 %copy.141 = bf16[128,192,128]{2,1,0:T(8,128)(2,1)} copy(bf16[128,192,128]{0,2,1:T(8,128)(2,1)} %bitcast.162) | data formatting | bytes 12582912 | tf_op jit(solution)/shard_map/reshape | solution.py:311
  335.2 6.4 %all-to-all-start.3 = ((bf16[128,192,128]{2,1,0:T(8,128)(2,1)}), bf16[128,192,128]{2,1,0:T(8,128)(2,1)}, u32[]{:S(2)}, u32[]{:S(2)}) async-start(bf16[128,192,128]{2,1,0:T(8,128)(2,1)} %copy.141), calls=%async_computation.4 | async-start | bytes 12582912 | tf_op jit(solution)/shard_map/all_to_all | solution.py:310
  341.9 2.8 fusion.26
  344.8 1.3 copy.143
  346.1 73.5 %all-to-all-done.3 = bf16[128,192,128]{2,1,0:T(8,128)(2,1)} async-done(((bf16[128,192,128]{2,1,0:T(8,128)(2,1)}), bf16[128,192,128]{2,1,0:T(8,128)(2,1)}, u32[]{:S(2)}, u32[]{:S(2)}) %all-to-all-start.3) | async-done | bytes 6291488 | tf_op jit(solution)/shard_map/all_to_all | solution.py:310
  419.6 11.2 %gather_fusion = bf16[1024,16,128]{2,1,0:T(8,128)(2,1)} fusion(bf16[1536,16,128]{2,1,0:T(8,128)(2,1)} %bitcast.57, s32[1024]{0:T(1024)S(1)} %broadcast_clamp_fusion), kind=kCustom, calls=%fused_computation | custom fusion | bytes 8392704 | tf_op jit(solution)/shard_map/gather | solution.py:317
  430.8 3.5 fusion.7
  434.3 1.1 fusion.41
  (84 shorter events, 5.9 us)
Async XLA Ops:
  7.2 303.3 %copy-start = (bf16[1,768,2048]{2,1,0:T(8,128)(2,1)S(1)}, bf16[1,768,2048]{2,1,0:T(8,128)(2,1)}, u32[]{:S(2)}) copy-start(bf16[1,768,2048]{2,1,0:T(8,128)(2,1)} %param.35) | copy-start | bytes 9437188
  7.2 8.9 %copy-start.8 = (s32[1,8]{1,0:T(1,128)S(1)}, s32[1,8]{1,0:T(1,128)}, u32[]{:S(2)}) copy-start(s32[1,8]{1,0:T(1,128)} %param.31) | copy-start | bytes 100
  7.2 9.0 %copy-start.10 = (f32[128]{0:T(128)S(1)}, f32[128]{0:T(128)}, u32[]{:S(2)}) copy-start(f32[128]{0:T(128)} %param.25) | copy-start | bytes 1540
  19.8 9.1 %copy-start.9 = (s32[8,1,2,1]{0,3,2,1:T(1,128)S(1)}, s32[8,1,2,1]{0,3,2,1:T(1,128)}, u32[]{:S(2)}) copy-start(s32[8,1,2,1]{0,3,2,1:T(1,128)} %param.37) | copy-start | bytes 196
  19.8 73.9 %all-to-all-start = ((bf16[32,320,256]{2,1,0:T(8,128)(2,1)}), bf16[32,320,256]{2,1,0:T(8,128)(2,1)}, u32[]{:S(2)}, u32[]{:S(2)}) async-start(bf16[32,320,256]{2,1,0:T(8,128)(2,1)} %broadcast_in_dim.151), calls=%async_computation | async-start | bytes 10485760 | tf_op jit(solution)/shard_map/all_to_all | solution.py:194
  28.8 145.9 %reduce-scatter.2.cloned.1.call-start = ((), (), s32[]{:S(2)}) async-start(), calls=%async_computation.5 | async-start | bytes 1572864 | tf_op jit(solution)/shard_map/reduce_scatter | solution.py:268
  30.9 11.9 %copy-start.3 = (s32[10240]{0:T(1024)}, s32[10240]{0:T(1024)S(1)}, u32[]{:S(2)}) copy-start(s32[10240]{0:T(1024)S(1)} %get-tuple-element.46) | copy-start | bytes 122884
  30.9 11.9 %copy-start.4 = (s32[10240]{0:T(1024)}, s32[10240]{0:T(1024)S(1)}, u32[]{:S(2)}) copy-start(s32[10240]{0:T(1024)S(1)} %get-tuple-element.47) | copy-start | bytes 122884
  35.7 7.0 %copy-start.12 = (f32[2048]{0:T(1024)S(1)}, f32[2048]{0:T(1024)}, u32[]{:S(2)}) copy-start(f32[2048]{0:T(1024)} %param.20) | copy-start | bytes 24580
  42.8 4.2 copy-start.11
  136.3 31.8 %copy-start.7 = (s32[1,128,8]{1,2,0:T(8,128)S(1)}, s32[1,128,8]{1,2,0:T(8,128)}, u32[]{:S(2)}) copy-start(s32[1,128,8]{1,2,0:T(8,128)} %param.32) | copy-start | bytes 12292
  136.4 40.7 %copy-start.6 = (f32[2048]{0:T(1024)S(1)}, f32[2048]{0:T(1024)}, u32[]{:S(2)}) copy-start(f32[2048]{0:T(1024)} %param.27) | copy-start | bytes 24580
  136.4 59.0 %all-to-all-start.1 = ((bf16[1,32,144,256]{3,2,0,1:T(8,128)(2,1)}), bf16[1,32,144,256]{3,2,0,1:T(8,128)(2,1)}, u32[]{:S(2)}, u32[]{:S(2)}) async-start(bf16[1,32,144,256]{3,2,0,1:T(8,128)(2,1)} %bitcast.165), calls=%async_computation.2 | async-start | bytes 4718592 | tf_op jit(solution)/shard_map/all_to_all | solution.py:234
  176.2 0.8 copy-start.1
  335.2 6.4 %copy-start.5 = (f32[1,128,8]{1,2,0:T(8,128)S(1)}, f32[1,128,8]{1,2,0:T(8,128)}, u32[]{:S(2)}) copy-start(f32[1,128,8]{1,2,0:T(8,128)} %param.33) | copy-start | bytes 12292
  335.2 84.3 %all-to-all-start.3 = ((bf16[128,192,128]{2,1,0:T(8,128)(2,1)}), bf16[128,192,128]{2,1,0:T(8,128)(2,1)}, u32[]{:S(2)}, u32[]{:S(2)}) async-start(bf16[128,192,128]{2,1,0:T(8,128)(2,1)} %copy.141), calls=%async_computation.4 | async-start | bytes 12582912 | tf_op jit(solution)/shard_map/all_to_all | solution.py:310
  430.8 3.5 copy-start.2
Sparse Core Ops, SparseCore 0:
  136.5 37.1 reduce-scatter.1
where the time goes:
time: 450 us; the launch traced here: 443 us
  waiting for transfers between devices  111 us (25%)
  blocking collectives  86.7 us (19%)
  local copies, waits for them, and re-layouts  81.2 us (18%)
  starting transfers between devices  47.2 us (10%)
  matrix products  45.5 us (10%)
  other arithmetic  29 us (6%)
  Pallas kernels  26.8 us (6%)
  between operations  14.8 us (3%)
    all_to_all x1, blocking collectives, shards(): lax.all_to_all(outgoing, moe_axes, split_axis=0, concat_axis=0, tiled=True)  86.7 us
    all_to_all x1, waiting for transfers between devices, shards(): lax.all_to_all(done.reshape(device_count, exp_local * capacity * chunks,...  73.5 us
    all_to_all x1, waiting for transfers between devices, shards(): lax.all_to_all(jnp.broadcast_to(local_kv[None], (seq_size,) + local_kv.sh...  34.6 us
    all_to_all x1, starting transfers between devices, shards(): lax.all_to_all(outgoing_pages, 'seq', split_axis=1, concat_axis=1, tiled=...  31.7 us
    pallas_call x1, Pallas kernels, flash_attention(): pl.pallas_call(functools.partial(flash_kernel, nkb, scale), grid_spec=gri...  26.8 us
    dot_general x1, matrix products, expert_mlp(): jnp.einsum('sejd,edf->sejf', arrived, w_gate_up, preferred_element_type=j...  14.5 us
    gather x1, local copies, waits for them, and re-layouts, shards(): gathered = returned.reshape(experts * capacity, chunks, lanes)[target]  11.2 us
    reshape x1, local copies, waits for them, and re-layouts, shards(): outgoing.reshape(device_count, exp_local * capacity * chunks, lanes)  10.4 us
  transfers between devices with their start and end apart: 4, of which 3 were waited for; matrix products, arithmetic and copies ran while one was open for 13% of the time, Pallas kernels for 0%

commit v1 on v0

--- a/solution.py
+++ b/solution.py
@@ -67,10 +67,7 @@
             q_ref[...], k_ref[...], (((1,), (1,)), ((), ())), preferred_element_type=jnp.float32
         ) * scale
         visible = (qreq_ref[...] == kreq_ref[...]) & (kpos_ref[...] <= qpos_ref[...])
-        heads = scores.shape[0] // visible.shape[0]
-        scores = jnp.where(
-            visible[None], scores.reshape((heads,) + visible.shape), -jnp.inf
-        ).reshape(scores.shape)
+        scores = jnp.where(visible, scores, -jnp.inf)
         m_old = m_sc[...]
         m_new = jnp.maximum(m_old, jnp.max(scores, axis=1, keepdims=True))
         expo = jnp.exp(scores - m_new)
@@ -122,10 +119,10 @@
 
 
 def expert_mlp(arrived, w_gate_up, w_down):
-    hidden = jnp.einsum("sejd,edf->sejf", arrived, w_gate_up, preferred_element_type=jnp.float32)
+    hidden = jnp.einsum("erd,edf->erf", arrived, w_gate_up, preferred_element_type=jnp.float32)
     inner = hidden.shape[-1] // 2
     act = (jax.nn.silu(hidden[..., :inner]) * hidden[..., inner:]).astype(jnp.bfloat16)
-    return jnp.einsum("sejf,efd->sejd", act, w_down, preferred_element_type=jnp.float32).astype(
+    return jnp.einsum("erf,efd->erd", act, w_down, preferred_element_type=jnp.float32).astype(
         jnp.bfloat16
     )
 
@@ -242,8 +239,8 @@
     seen = (query_req[:, None] == key_req[None, :]) & (key_pos[None, :] <= query_pos[:, None])
     live = jnp.any(jnp.any(seen, axis=0).reshape(length // KEY_BLOCK, KEY_BLOCK), axis=1).astype(jnp.int32)
     rows = group * tok_count
-    qreq_rows = query_req.reshape(tok_count, 1)
-    qpos_rows = query_pos.reshape(tok_count, 1)
+    qreq_rows = jnp.broadcast_to(query_req[None, :], (group, tok_count)).reshape(rows, 1)
+    qpos_rows = jnp.broadcast_to(query_pos[None, :], (group, tok_count)).reshape(rows, 1)
     heads_out = []
     for h in range(kv_local):
         heads_out.append(
@@ -306,7 +303,16 @@
         (outgoing, arrived_pages, arrived_slots)
     )
     arrived = lax.all_to_all(outgoing, moe_axes, split_axis=0, concat_axis=0, tiled=True)
-    done = expert_mlp(arrived.reshape(device_count, exp_local, capacity, width), w_gate_up, w_down)
+    expert_rows = (
+        arrived.reshape(device_count, exp_local, capacity, width)
+        .transpose(1, 0, 2, 3)
+        .reshape(exp_local, device_count * capacity, width)
+    )
+    done = expert_mlp(expert_rows, w_gate_up, w_down)
+    done = (
+        done.reshape(exp_local, device_count, capacity, width)
+        .transpose(1, 0, 2, 3)
+    )
     returned = lax.all_to_all(
         done.reshape(device_count, exp_local * capacity * chunks, lanes),
         moe_axes,

time: 450 us -> 431 us (0.958)
  starting transfers between devices: 47.2 us -> 38.3 us
  local copies, waits for them, and re-layouts: 81.2 us -> 76.4 us
    another operation x0 -> x2, local copies, waits for them, and re-layouts: none -> 20.8 us  [the longest x1 10.5 us: shards(): done.reshape(device_count, exp_local * capacity * chunks, lanes)]
    all_to_all x1 -> x0, local copies, waits for them, and re-layouts: 9.23 us -> none  [shards(): lax.all_to_all(outgoing, moe_axes, split_axis=0, concat_axis=0, tiled=True)]
    reshape x1 -> x0, local copies, waits for them, and re-layouts: 9.03 us -> none  [shards(): done.reshape(device_count, exp_local * capacity * chunks, lanes)]
    convert_element_type x1 -> x0, local copies, waits for them, and re-layouts: 8.66 us -> none  [expert_mlp(): jnp.einsum('sejf,efd->sejd', act, w_down, preferred_element_type=jnp.floa...]
    all_to_all x1, starting transfers between devices: 31.7 us -> 23.3 us  [shards(): lax.all_to_all(outgoing_pages, 'seq', split_axis=1, concat_axis=1, tiled=...]
  transfers between devices with their start and end apart: 4 -> 4, of which waited for: 3 -> 3; matrix products, arithmetic and copies ran while one was open for 13% -> 14% of each run, Pallas kernels for 0% -> 0%
where the time goes in v1:
time: 431 us; the launch traced here: 425 us
  waiting for transfers between devices  112 us (26%)
  blocking collectives  86.5 us (20%)
  local copies, waits for them, and re-layouts  76.4 us (18%)
  matrix products  45.1 us (10%)
  starting transfers between devices  38.3 us (9%)
  other arithmetic  28.3 us (7%)
  Pallas kernels  23.5 us (5%)
  between operations  15 us (3%)
    all_to_all x1, blocking collectives, shards(): lax.all_to_all(outgoing, moe_axes, split_axis=0, concat_axis=0, tiled=True)  86.5 us
    all_to_all x1, waiting for transfers between devices, shards(): lax.all_to_all(done.reshape(device_count, exp_local * capacity * chunks,...  74.2 us
    all_to_all x1, waiting for transfers between devices, shards(): lax.all_to_all(jnp.broadcast_to(local_kv[None], (seq_size,) + local_kv.sh...  34.5 us
    pallas_call x1, Pallas kernels, flash_attention(): pl.pallas_call(functools.partial(flash_kernel, nkb, scale), grid_spec=gri...  23.5 us
    all_to_all x1, starting transfers between devices, shards(): lax.all_to_all(outgoing_pages, 'seq', split_axis=1, concat_axis=1, tiled=...  23.3 us
    dot_general x1, matrix products, expert_mlp(): jnp.einsum('erd,edf->erf', arrived, w_gate_up, preferred_element_type=jnp...  14.1 us
    gather x1, local copies, waits for them, and re-layouts, shards(): gathered = returned.reshape(experts * capacity, chunks, lanes)[target]  11.2 us
    another operation x1, local copies, waits for them, and re-layouts, shards(): done.reshape(device_count, exp_local * capacity * chunks, lanes)  10.5 us
  transfers between devices with their start and end apart: 4, of which 3 were waited for; matrix products, arithmetic and copies ran while one was open for 14% of the time, Pallas kernels for 0%

profile of v1, /device:TPU:25, one launch (start us, length us, event | category | flops | bytes accessed | tf_op | source)
XLA Modules:
  0.0 425.4 jit_solution(16532179000517204778)
XLA Ops:
  7.2 1.0 reduce-window.6
  8.2 0.7 fusion.67
  8.9 1.5 fusion.12
  10.4 0.8 copy.88
  11.2 0.8 copy.89
  12.1 2.0 convolution_convert_fusion.3
  14.0 2.0 multiply_reduce_fusion.1
  16.9 2.9 broadcast_in_dim.162
  19.8 9.0 %all-to-all-start = ((bf16[32,320,256]{2,1,0:T(8,128)(2,1)}), bf16[32,320,256]{2,1,0:T(8,128)(2,1)}, u32[]{:S(2)}, u32[]{:S(2)}) async-start(bf16[32,320,256]{2,1,0:T(8,128)(2,1)} %broadcast_in_dim.162), calls=%async_computation | async-start | bytes 10485760 | tf_op jit(solution)/shard_map/all_to_all | solution.py:191
  31.0 3.0 and_reduce_fusion
  34.7 1.3 copy.107
  36.0 1.4 copy.109
  37.4 6.7 %copy.105 = bf16[1024,2048]{1,0:T(8,128)(2,1)} copy(bf16[1024,2048]{0,1:T(8,128)(2,1)} %bitcast.158) | data formatting | bytes 8388608 | tf_op jit(solution)/shard_map/dot_general | solution.py:162
  44.1 3.9 multiply_reduce_fusion
  48.7 0.8 maximum_bitcast_fusion
  49.5 2.1 copy.84
  51.6 1.5 broadcast.441
  53.1 3.4 scatter_fusion
  56.6 3.2 pad_maximum_fusion.1
  59.8 34.5 %all-to-all-done = bf16[32,320,256]{2,1,0:T(8,128)(2,1)} async-done(((bf16[32,320,256]{2,1,0:T(8,128)(2,1)}), bf16[32,320,256]{2,1,0:T(8,128)(2,1)}, u32[]{:S(2)}, u32[]{:S(2)}) %all-to-all-start) | async-done | bytes 5242912 | tf_op jit(solution)/shard_map/all_to_all | solution.py:191
  94.4 1.3 slice.40
  95.7 2.5 slice.41
  98.1 5.4 %pad_maximum_fusion = (bf16[10240,128]{1,0:T(8,128)(2,1)}, bf16[10240,128]{1,0:T(8,128)(2,1)}) fusion(bf16[8192,256]{1,0:T(8,128)(2,1)S(1)} %bitcast.153, bf16[2048,256]{1,0:T(8,128)(2,1)S(1)} %bitcast.157), kind=kLoop, calls=%fused_computation.24 | loop fusion | flops 10485760 | bytes 10485760 | tf_op jit(solution)/shard_map/concatenate | solution.py:234
  103.5 23.5 %shard_map.194 = bf16[2048,128]{1,0:T(8,128)(2,1)} custom-call(s32[20]{0:T(128)} %convert_element_type.156.live_ref, s32[2048,1]{1,0:T(8,128)} %bitcast.162, s32[2048,1]{1,0:T(8,128)} %bitcast.163, s32[1,10240]{1,0:T(1,128)} %bitcast.168, s32[1,10240]{1,0:T(1,128)} %bitcast.169, bf16[2048,128]{1,0:T(8,128)(2,1)} %bitcast.165, ...), custom_call_target="tpu_custom_call" | custom-call | flops 10737418240 | bytes 6291456 | tf_op jit(solution)/shard_map/pallas_call | solution.py:110
  127.0 2.0 copy.94
  129.1 4.6 %convolution_convert_fusion.2 = bf16[256,2048]{1,0:T(8,128)(2,1)} fusion(bf16[256,1024]{0,1:T(8,128)(2,1)} %bitcast.167, bf16[1024,2048]{1,0:T(8,128)(2,1)} %param.26), kind=kOutput, calls=%fused_computation.25 | convolution fusion | flops 1074266112 | bytes 5767168 | tf_op jit(solution)/shard_map/dot_general | solution.py:266
  133.7 23.3 %all-to-all-start.1 = ((bf16[1,32,144,256]{3,2,0,1:T(8,128)(2,1)}), bf16[1,32,144,256]{3,2,0,1:T(8,128)(2,1)}, u32[]{:S(2)}, u32[]{:S(2)}) async-start(bf16[1,32,144,256]{3,2,0,1:T(8,128)(2,1)} %bitcast.155), calls=%async_computation.2 | async-start | bytes 4718592 | tf_op jit(solution)/shard_map/all_to_all | solution.py:231
  157.2 0.6 fusion.26
  158.0 5.6 %fusion.1 = pred[1536,128]{1,0:T(8,128)(4,1)S(1)} fusion(s32[128,8]{0,1:T(8,128)S(1)} %copy.97), kind=kLoop, calls=%fused_computation.9 | loop fusion | flops 2949120 | bytes 200704 | tf_op jit(solution)/shard_map/reduce_or | solution.py:299
  163.6 1.5 fusion.27
  165.1 0.8 copy-done.1
  165.9 4.5 %convolution_convert_fusion.1 = bf16[1536,2048]{1,0:T(8,128)(2,1)} fusion(pred[1536,128]{1,0:T(8,128)(4,1)S(1)} %fusion.1, bf16[128,2048]{1,0:T(8,128)(2,1)S(1)} %get-tuple-element.27, f32[2048]{0:T(1024)S(1)} %copy-done.6, f32[128]{0:T(128)S(1)} %add_rsqrt_fusion.3), kind=kOutput, calls=%fused_computation.6 | convolution fusion | flops 809500672 | bytes 7021056 | tf_op jit(solution)/shard_map/dot_general | solution.py:300
  170.4 10.4 %reshape.741 = bf16[128,192,128]{2,1,0:T(8,128)(2,1)} reshape(bf16[1536,2048]{1,0:T(8,128)(2,1)} %convolution_convert_fusion.1) | data formatting | bytes 12582912 | tf_op jit(solution)/shard_map/reshape | solution.py:301
  180.9 3.5 all-to-all-done.1
  184.3 1.5 fusion.58
  185.8 3.2 slice.60
  189.0 86.5 %all_to_all.20 = bf16[128,192,128]{2,1,0:T(8,128)(2,1)} all-to-all(bf16[128,192,128]{2,1,0:T(8,128)(2,1)} %reshape.741), channel_id=1, replica_groups=mesh['seq'=32,'tp'=2,'pd'=2] {'seq','tp','pd'}, dimensions={0} | all-to-all | bytes 12582912 | tf_op jit(solution)/shard_map/all_to_all | solution.py:305
  275.5 10.3 %reshape.742 = bf16[1536,2048]{1,0:T(8,128)(2,1)} reshape(bf16[128,192,128]{2,1,0:T(8,128)(2,1)} %all_to_all.20) | data formatting | bytes 12582912 | tf_op jit(solution)/shard_map/reshape.32
  285.8 14.1 %convolution_bitcast_fusion = f32[1,1536,1536]{2,1,0:T(8,128)S(1)} fusion(bf16[1536,2048]{1,0:T(8,128)(2,1)} %reshape.742, bf16[1,2048,1536]{2,1,0:T(8,128)(2,1)} %param.34), kind=kOutput, calls=%fused_computation.4 | convolution fusion | flops 9663676416 | bytes 22020096 | tf_op jit(solution)/shard_map/erd,edf->erf/dot_general | solution.py:122
  300.0 7.1 %convolution_convert_fusion = bf16[1536,2048]{1,0:T(8,128)(2,1)} fusion(bf16[1,768,2048]{2,1,0:T(8,128)(2,1)S(1)} %copy-done, f32[1,1536,1536]{2,1,0:T(8,128)S(1)} %convolution_bitcast_fusion), kind=kOutput, calls=%fused_computation.5 | convolution fusion | flops 4842061824 | bytes 18874368 | tf_op jit(solution)/shard_map/erf,efd->erd/dot_general | solution.py:125
  307.0 10.5 %reshape_transpose_reshape.4 = bf16[128,192,128]{2,1,0:T(8,128)(2,1)} reshape(bf16[1536,2048]{1,0:T(8,128)(2,1)} %convolution_convert_fusion) | data formatting | bytes 12582912 | tf_op jit(solution)/shard_map/reshape;transpose;reshape | solution.py:317
  317.5 5.9 %all-to-all-start.3 = ((bf16[128,192,128]{2,1,0:T(8,128)(2,1)}), bf16[128,192,128]{2,1,0:T(8,128)(2,1)}, u32[]{:S(2)}, u32[]{:S(2)}) async-start(bf16[128,192,128]{2,1,0:T(8,128)(2,1)} %reshape_transpose_reshape.4), calls=%async_computation.4 | async-start | bytes 12582912 | tf_op jit(solution)/shard_map/all_to_all | solution.py:316
  323.7 2.8 fusion.22
  326.6 1.3 copy.100
  327.9 74.2 %all-to-all-done.3 = bf16[128,192,128]{2,1,0:T(8,128)(2,1)} async-done(((bf16[128,192,128]{2,1,0:T(8,128)(2,1)}), bf16[128,192,128]{2,1,0:T(8,128)(2,1)}, u32[]{:S(2)}, u32[]{:S(2)}) %all-to-all-start.3) | async-done | bytes 6291488 | tf_op jit(solution)/shard_map/all_to_all | solution.py:316
  402.2 11.2 %gather_fusion = bf16[1024,16,128]{2,1,0:T(8,128)(2,1)} fusion(bf16[1536,16,128]{2,1,0:T(8,128)(2,1)} %bitcast.43, s32[1024]{0:T(1024)S(1)} %broadcast_clamp_fusion), kind=kCustom, calls=%fused_computation | custom fusion | bytes 8392704 | tf_op jit(solution)/shard_map/gather | solution.py:323
  413.4 3.5 fusion.3
  416.9 1.1 fusion.37
  (85 shorter events, 5.1 us)
Async XLA Ops:
  7.2 292.8 %copy-start = (bf16[1,768,2048]{2,1,0:T(8,128)(2,1)S(1)}, bf16[1,768,2048]{2,1,0:T(8,128)(2,1)}, u32[]{:S(2)}) copy-start(bf16[1,768,2048]{2,1,0:T(8,128)(2,1)} %param.35) | copy-start | bytes 9437188
  7.2 8.9 %copy-start.8 = (s32[1,8]{1,0:T(1,128)S(1)}, s32[1,8]{1,0:T(1,128)}, u32[]{:S(2)}) copy-start(s32[1,8]{1,0:T(1,128)} %param.31) | copy-start | bytes 100
  7.2 9.0 %copy-start.10 = (f32[128]{0:T(128)S(1)}, f32[128]{0:T(128)}, u32[]{:S(2)}) copy-start(f32[128]{0:T(128)} %param.25) | copy-start | bytes 1540
  19.8 9.1 %copy-start.9 = (s32[8,1,2,1]{0,3,2,1:T(1,128)S(1)}, s32[8,1,2,1]{0,3,2,1:T(1,128)}, u32[]{:S(2)}) copy-start(s32[8,1,2,1]{0,3,2,1:T(1,128)} %param.37) | copy-start | bytes 196
  19.8 74.6 %all-to-all-start = ((bf16[32,320,256]{2,1,0:T(8,128)(2,1)}), bf16[32,320,256]{2,1,0:T(8,128)(2,1)}, u32[]{:S(2)}, u32[]{:S(2)}) async-start(bf16[32,320,256]{2,1,0:T(8,128)(2,1)} %broadcast_in_dim.162), calls=%async_computation | async-start | bytes 10485760 | tf_op jit(solution)/shard_map/all_to_all | solution.py:191
  28.8 134.8 %reduce-scatter.2.cloned.1.call-start = ((), (), s32[]{:S(2)}) async-start(), calls=%async_computation.5 | async-start | bytes 1572864 | tf_op jit(solution)/shard_map/reduce_scatter | solution.py:265
  31.0 13.1 %copy-start.3 = (s32[10240]{0:T(1024)}, s32[10240]{0:T(1024)S(1)}, u32[]{:S(2)}) copy-start(s32[10240]{0:T(1024)S(1)} %get-tuple-element.44) | copy-start | bytes 122884
  31.0 13.1 %copy-start.4 = (s32[10240]{0:T(1024)}, s32[10240]{0:T(1024)S(1)}, u32[]{:S(2)}) copy-start(s32[10240]{0:T(1024)S(1)} %get-tuple-element.45) | copy-start | bytes 122884
  37.4 6.7 %copy-start.12 = (f32[2048]{0:T(1024)S(1)}, f32[2048]{0:T(1024)}, u32[]{:S(2)}) copy-start(f32[2048]{0:T(1024)} %param.20) | copy-start | bytes 24580
  44.1 4.2 copy-start.11
  133.6 23.3 %copy-start.7 = (s32[1,128,8]{1,2,0:T(8,128)S(1)}, s32[1,128,8]{1,2,0:T(8,128)}, u32[]{:S(2)}) copy-start(s32[1,128,8]{1,2,0:T(8,128)} %param.32) | copy-start | bytes 12292
  133.7 32.2 %copy-start.6 = (f32[2048]{0:T(1024)S(1)}, f32[2048]{0:T(1024)}, u32[]{:S(2)}) copy-start(f32[2048]{0:T(1024)} %param.27) | copy-start | bytes 24580
  133.7 50.6 %all-to-all-start.1 = ((bf16[1,32,144,256]{3,2,0,1:T(8,128)(2,1)}), bf16[1,32,144,256]{3,2,0,1:T(8,128)(2,1)}, u32[]{:S(2)}, u32[]{:S(2)}) async-start(bf16[1,32,144,256]{3,2,0,1:T(8,128)(2,1)} %bitcast.155), calls=%async_computation.2 | async-start | bytes 4718592 | tf_op jit(solution)/shard_map/all_to_all | solution.py:231
  165.1 0.8 copy-start.1
  317.5 6.0 %copy-start.5 = (f32[1,128,8]{1,2,0:T(8,128)S(1)}, f32[1,128,8]{1,2,0:T(8,128)}, u32[]{:S(2)}) copy-start(f32[1,128,8]{1,2,0:T(8,128)} %param.33) | copy-start | bytes 12292
  317.5 84.7 %all-to-all-start.3 = ((bf16[128,192,128]{2,1,0:T(8,128)(2,1)}), bf16[128,192,128]{2,1,0:T(8,128)(2,1)}, u32[]{:S(2)}, u32[]{:S(2)}) async-start(bf16[128,192,128]{2,1,0:T(8,128)(2,1)} %reshape_transpose_reshape.4), calls=%async_computation.4 | async-start | bytes 12582912 | tf_op jit(solution)/shard_map/all_to_all | solution.py:316
  413.4 3.5 copy-start.2
Sparse Core Ops, SparseCore 0:
  133.8 28.1 reduce-scatter.1

commit v2 on v1

--- a/solution.py
+++ b/solution.py
@@ -61,13 +61,13 @@
         l_sc[...] = jnp.zeros(l_sc.shape, jnp.float32)
         acc_sc[...] = jnp.zeros(acc_sc.shape, jnp.float32)
 
-    @pl.when(live_ref[kb] > 0)
-    def _():
+    def accumulate(masked):
         scores = lax.dot_general(
             q_ref[...], k_ref[...], (((1,), (1,)), ((), ())), preferred_element_type=jnp.float32
         ) * scale
-        visible = (qreq_ref[...] == kreq_ref[...]) & (kpos_ref[...] <= qpos_ref[...])
-        scores = jnp.where(visible, scores, -jnp.inf)
+        if masked:
+            visible = (qreq_ref[...] == kreq_ref[...]) & (kpos_ref[...] <= qpos_ref[...])
+            scores = jnp.where(visible, scores, -jnp.inf)
         m_old = m_sc[...]
         m_new = jnp.maximum(m_old, jnp.max(scores, axis=1, keepdims=True))
         expo = jnp.exp(scores - m_new)
@@ -77,6 +77,14 @@
             expo.astype(jnp.bfloat16), v_ref[...], preferred_element_type=jnp.float32
         )
         m_sc[...] = m_new
+
+    @pl.when(live_ref[kb] == 1)
+    def _():
+        accumulate(True)
+
+    @pl.when(live_ref[kb] == 2)
+    def _():
+        accumulate(False)
 
     @pl.when(kb == nkb - 1)
     def _():
@@ -237,7 +245,9 @@
     )
     length = ordered_kv.shape[0]
     seen = (query_req[:, None] == key_req[None, :]) & (key_pos[None, :] <= query_pos[:, None])
-    live = jnp.any(jnp.any(seen, axis=0).reshape(length // KEY_BLOCK, KEY_BLOCK), axis=1).astype(jnp.int32)
+    some_seen = jnp.any(jnp.any(seen, axis=0).reshape(length // KEY_BLOCK, KEY_BLOCK), axis=1)
+    all_seen = jnp.all(jnp.all(seen, axis=0).reshape(length // KEY_BLOCK, KEY_BLOCK), axis=1)
+    live = jnp.where(all_seen, 2, jnp.where(some_seen, 1, 0)).astype(jnp.int32)
     rows = group * tok_count
     qreq_rows = jnp.broadcast_to(query_req[None, :], (group, tok_count)).reshape(rows, 1)
     qpos_rows = jnp.broadcast_to(query_pos[None, :], (group, tok_count)).reshape(rows, 1)

time: 431 us -> 435 us (level)
  no operation moved by 1% of the time
where the time goes in v2:
time: 435 us; the launch traced here: 430 us
  waiting for transfers between devices  112 us (26%)
  blocking collectives  86.6 us (20%)
  local copies, waits for them, and re-layouts  76.8 us (18%)
  matrix products  45.1 us (10%)
  starting transfers between devices  39.2 us (9%)
  other arithmetic  27.9 us (6%)
  Pallas kernels  26.7 us (6%)
  between operations  14.8 us (3%)
    all_to_all x1, blocking collectives, shards(): lax.all_to_all(outgoing, moe_axes, split_axis=0, concat_axis=0, tiled=True)  86.6 us
    all_to_all x1, waiting for transfers between devices, shards(): lax.all_to_all(done.reshape(device_count, exp_local * capacity * chunks,...  74.2 us
    all_to_all x1, waiting for transfers between devices, shards(): lax.all_to_all(jnp.broadcast_to(local_kv[None], (seq_size,) + local_kv.sh...  34.7 us
    pallas_call x1, Pallas kernels, flash_attention(): pl.pallas_call(functools.partial(flash_kernel, nkb, scale), grid_spec=gri...  26.7 us
    all_to_all x1, starting transfers between devices, shards(): lax.all_to_all(outgoing_pages, 'seq', split_axis=1, concat_axis=1, tiled=...  24.3 us
    dot_general x1, matrix products, expert_mlp(): jnp.einsum('erd,edf->erf', arrived, w_gate_up, preferred_element_type=jnp...  14.1 us
    gather x1, local copies, waits for them, and re-layouts, shards(): gathered = returned.reshape(experts * capacity, chunks, lanes)[target]  11.2 us
    another operation x1, local copies, waits for them, and re-layouts, shards(): done.reshape(device_count, exp_local * capacity * chunks, lanes)  10.5 us
  transfers between devices with their start and end apart: 4, of which 3 were waited for; matrix products, arithmetic and copies ran while one was open for 14% of the time, Pallas kernels for 0%

profile of v2, /device:TPU:25, one launch (start us, length us, event | category | flops | bytes accessed | tf_op | source)
XLA Modules:
  0.0 429.6 jit_solution(8998951383550993758)
XLA Ops:
  7.2 1.0 reduce-window.6
  8.2 0.7 fusion.69
  8.9 1.5 fusion.14
  10.4 0.8 copy.88
  11.2 0.8 copy.89
  12.1 2.0 convolution_convert_fusion.3
  14.0 2.0 multiply_reduce_fusion.1
  16.9 2.9 broadcast_in_dim.177
  19.8 9.0 %all-to-all-start = ((bf16[32,320,256]{2,1,0:T(8,128)(2,1)}), bf16[32,320,256]{2,1,0:T(8,128)(2,1)}, u32[]{:S(2)}, u32[]{:S(2)}) async-start(bf16[32,320,256]{2,1,0:T(8,128)(2,1)} %broadcast_in_dim.177), calls=%async_computation | async-start | bytes 10485760 | tf_op jit(solution)/shard_map/all_to_all | solution.py:199
  29.6 1.1 scatter_custom_fusion.1
  31.5 2.4 fusion
  34.0 1.3 copy.107
  35.3 1.4 copy.109
  36.7 6.5 %copy.105 = bf16[1024,2048]{1,0:T(8,128)(2,1)} copy(bf16[1024,2048]{0,1:T(8,128)(2,1)} %bitcast.158) | data formatting | bytes 8388608 | tf_op jit(solution)/shard_map/dot_general | solution.py:170
  43.3 3.9 multiply_reduce_fusion
  47.9 0.8 maximum_bitcast_fusion
  48.7 2.1 copy.84
  51.0 1.5 broadcast.447
  52.5 3.4 scatter_fusion
  56.0 3.2 pad_maximum_fusion.1
  59.8 34.7 %all-to-all-done = bf16[32,320,256]{2,1,0:T(8,128)(2,1)} async-done(((bf16[32,320,256]{2,1,0:T(8,128)(2,1)}), bf16[32,320,256]{2,1,0:T(8,128)(2,1)}, u32[]{:S(2)}, u32[]{:S(2)}) %all-to-all-start) | async-done | bytes 5242912 | tf_op jit(solution)/shard_map/all_to_all | solution.py:199
  94.5 1.3 slice.40
  95.8 2.5 slice.41
  98.2 5.4 %pad_maximum_fusion = (bf16[10240,128]{1,0:T(8,128)(2,1)}, bf16[10240,128]{1,0:T(8,128)(2,1)}) fusion(bf16[8192,256]{1,0:T(8,128)(2,1)S(1)} %bitcast.153, bf16[2048,256]{1,0:T(8,128)(2,1)S(1)} %bitcast.157), kind=kLoop, calls=%fused_computation.26 | loop fusion | flops 10485760 | bytes 10485760 | tf_op jit(solution)/shard_map/concatenate | solution.py:242
  103.6 26.7 %shard_map.194 = bf16[2048,128]{1,0:T(8,128)(2,1)} custom-call(s32[20]{0:T(128)} %select_select_fusion.live_ref, s32[2048,1]{1,0:T(8,128)} %bitcast.162, s32[2048,1]{1,0:T(8,128)} %bitcast.163, s32[1,10240]{1,0:T(1,128)} %bitcast.168, s32[1,10240]{1,0:T(1,128)} %bitcast.169, bf16[2048,128]{1,0:T(8,128)(2,1)} %bitcast.165, ...), custom_call_target="tpu_custom_call" | custom-call | flops 10737418240 | bytes 6291456 | tf_op jit(solution)/shard_map/pallas_call | solution.py:118
  130.3 2.0 copy.94
  132.4 4.6 %convolution_convert_fusion.2 = bf16[256,2048]{1,0:T(8,128)(2,1)} fusion(bf16[256,1024]{0,1:T(8,128)(2,1)} %bitcast.167, bf16[1024,2048]{1,0:T(8,128)(2,1)} %param.26), kind=kOutput, calls=%fused_computation.27 | convolution fusion | flops 1074266112 | bytes 5767168 | tf_op jit(solution)/shard_map/dot_general | solution.py:276
  137.0 24.3 %all-to-all-start.1 = ((bf16[1,32,144,256]{3,2,0,1:T(8,128)(2,1)}), bf16[1,32,144,256]{3,2,0,1:T(8,128)(2,1)}, u32[]{:S(2)}, u32[]{:S(2)}) async-start(bf16[1,32,144,256]{3,2,0,1:T(8,128)(2,1)} %bitcast.155), calls=%async_computation.2 | async-start | bytes 4718592 | tf_op jit(solution)/shard_map/all_to_all | solution.py:239
  162.3 5.6 %fusion.3 = pred[1536,128]{1,0:T(8,128)(4,1)S(1)} fusion(s32[128,8]{0,1:T(8,128)S(1)} %copy.97), kind=kLoop, calls=%fused_computation.11 | loop fusion | flops 2949120 | bytes 200704 | tf_op jit(solution)/shard_map/reduce_or | solution.py:309
  167.9 1.5 fusion.29
  169.4 0.8 copy-done.1
  170.2 4.5 %convolution_convert_fusion.1 = bf16[1536,2048]{1,0:T(8,128)(2,1)} fusion(pred[1536,128]{1,0:T(8,128)(4,1)S(1)} %fusion.3, bf16[128,2048]{1,0:T(8,128)(2,1)S(1)} %get-tuple-element.29, f32[2048]{0:T(1024)S(1)} %copy-done.6, f32[128]{0:T(128)S(1)} %add_rsqrt_fusion.3), kind=kOutput, calls=%fused_computation.8 | convolution fusion | flops 809500672 | bytes 7021056 | tf_op jit(solution)/shard_map/dot_general | solution.py:310
  174.7 10.4 %reshape.745 = bf16[128,192,128]{2,1,0:T(8,128)(2,1)} reshape(bf16[1536,2048]{1,0:T(8,128)(2,1)} %convolution_convert_fusion.1) | data formatting | bytes 12582912 | tf_op jit(solution)/shard_map/reshape | solution.py:311
  185.1 3.4 all-to-all-done.1
  188.5 1.5 fusion.60
  190.0 3.2 slice.60
  193.2 86.6 %all_to_all.20 = bf16[128,192,128]{2,1,0:T(8,128)(2,1)} all-to-all(bf16[128,192,128]{2,1,0:T(8,128)(2,1)} %reshape.745), channel_id=1, replica_groups=mesh['seq'=32,'tp'=2,'pd'=2] {'seq','tp','pd'}, dimensions={0} | all-to-all | bytes 12582912 | tf_op jit(solution)/shard_map/all_to_all | solution.py:315
  279.9 10.3 %reshape.746 = bf16[1536,2048]{1,0:T(8,128)(2,1)} reshape(bf16[128,192,128]{2,1,0:T(8,128)(2,1)} %all_to_all.20) | data formatting | bytes 12582912 | tf_op jit(solution)/shard_map/reshape.16
  290.2 14.1 %convolution_bitcast_fusion = f32[1,1536,1536]{2,1,0:T(8,128)S(1)} fusion(bf16[1536,2048]{1,0:T(8,128)(2,1)} %reshape.746, bf16[1,2048,1536]{2,1,0:T(8,128)(2,1)} %param.34), kind=kOutput, calls=%fused_computation.4 | convolution fusion | flops 9663676416 | bytes 22020096 | tf_op jit(solution)/shard_map/erd,edf->erf/dot_general | solution.py:130
  304.3 7.1 %convolution_convert_fusion = bf16[1536,2048]{1,0:T(8,128)(2,1)} fusion(bf16[1,768,2048]{2,1,0:T(8,128)(2,1)S(1)} %copy-done, f32[1,1536,1536]{2,1,0:T(8,128)S(1)} %convolution_bitcast_fusion), kind=kOutput, calls=%fused_computation.7 | convolution fusion | flops 4842061824 | bytes 18874368 | tf_op jit(solution)/shard_map/erf,efd->erd/dot_general | solution.py:133
  311.4 10.5 %reshape_transpose_reshape.4 = bf16[128,192,128]{2,1,0:T(8,128)(2,1)} reshape(bf16[1536,2048]{1,0:T(8,128)(2,1)} %convolution_convert_fusion) | data formatting | bytes 12582912 | tf_op jit(solution)/shard_map/reshape;transpose;reshape | solution.py:327
  321.9 5.9 %all-to-all-start.3 = ((bf16[128,192,128]{2,1,0:T(8,128)(2,1)}), bf16[128,192,128]{2,1,0:T(8,128)(2,1)}, u32[]{:S(2)}, u32[]{:S(2)}) async-start(bf16[128,192,128]{2,1,0:T(8,128)(2,1)} %reshape_transpose_reshape.4), calls=%async_computation.4 | async-start | bytes 12582912 | tf_op jit(solution)/shard_map/all_to_all | solution.py:326
  328.1 2.8 fusion.24
  331.0 1.3 copy.100
  332.3 74.2 %all-to-all-done.3 = bf16[128,192,128]{2,1,0:T(8,128)(2,1)} async-done(((bf16[128,192,128]{2,1,0:T(8,128)(2,1)}), bf16[128,192,128]{2,1,0:T(8,128)(2,1)}, u32[]{:S(2)}, u32[]{:S(2)}) %all-to-all-start.3) | async-done | bytes 6291488 | tf_op jit(solution)/shard_map/all_to_all | solution.py:326
  406.5 11.2 %gather_fusion = bf16[1024,16,128]{2,1,0:T(8,128)(2,1)} fusion(bf16[1536,16,128]{2,1,0:T(8,128)(2,1)} %bitcast.43, s32[1024]{0:T(1024)S(1)} %broadcast_clamp_fusion), kind=kCustom, calls=%fused_computation | custom fusion | bytes 8392704 | tf_op jit(solution)/shard_map/gather | solution.py:333
  417.8 3.5 fusion.5
  421.3 1.1 fusion.39
  (87 shorter events, 5.2 us)
Async XLA Ops:
  7.2 297.2 %copy-start = (bf16[1,768,2048]{2,1,0:T(8,128)(2,1)S(1)}, bf16[1,768,2048]{2,1,0:T(8,128)(2,1)}, u32[]{:S(2)}) copy-start(bf16[1,768,2048]{2,1,0:T(8,128)(2,1)} %param.35) | copy-start | bytes 9437188
  7.2 8.9 %copy-start.8 = (s32[1,8]{1,0:T(1,128)S(1)}, s32[1,8]{1,0:T(1,128)}, u32[]{:S(2)}) copy-start(s32[1,8]{1,0:T(1,128)} %param.31) | copy-start | bytes 100
  7.2 9.0 %copy-start.10 = (f32[128]{0:T(128)S(1)}, f32[128]{0:T(128)}, u32[]{:S(2)}) copy-start(f32[128]{0:T(128)} %param.25) | copy-start | bytes 1540
  19.8 9.1 %copy-start.9 = (s32[8,1,2,1]{0,3,2,1:T(1,128)S(1)}, s32[8,1,2,1]{0,3,2,1:T(1,128)}, u32[]{:S(2)}) copy-start(s32[8,1,2,1]{0,3,2,1:T(1,128)} %param.37) | copy-start | bytes 196
  19.8 74.7 %all-to-all-start = ((bf16[32,320,256]{2,1,0:T(8,128)(2,1)}), bf16[32,320,256]{2,1,0:T(8,128)(2,1)}, u32[]{:S(2)}, u32[]{:S(2)}) async-start(bf16[32,320,256]{2,1,0:T(8,128)(2,1)} %broadcast_in_dim.177), calls=%async_computation | async-start | bytes 10485760 | tf_op jit(solution)/shard_map/all_to_all | solution.py:199
  28.8 139.1 %reduce-scatter.2.cloned.1.call-start = ((), (), s32[]{:S(2)}) async-start(), calls=%async_computation.5 | async-start | bytes 1572864 | tf_op jit(solution)/shard_map/reduce_scatter | solution.py:275
  31.5 11.7 %copy-start.3 = (s32[10240]{0:T(1024)}, s32[10240]{0:T(1024)S(1)}, u32[]{:S(2)}) copy-start(s32[10240]{0:T(1024)S(1)} %get-tuple-element.46) | copy-start | bytes 122884
  31.5 11.7 %copy-start.4 = (s32[10240]{0:T(1024)}, s32[10240]{0:T(1024)S(1)}, u32[]{:S(2)}) copy-start(s32[10240]{0:T(1024)S(1)} %get-tuple-element.47) | copy-start | bytes 122884
  36.7 6.5 %copy-start.12 = (f32[2048]{0:T(1024)S(1)}, f32[2048]{0:T(1024)}, u32[]{:S(2)}) copy-start(f32[2048]{0:T(1024)} %param.20) | copy-start | bytes 24580
  43.2 4.2 copy-start.11
  137.0 24.3 %copy-start.7 = (s32[1,128,8]{1,2,0:T(8,128)S(1)}, s32[1,128,8]{1,2,0:T(8,128)}, u32[]{:S(2)}) copy-start(s32[1,128,8]{1,2,0:T(8,128)} %param.32) | copy-start | bytes 12292
  137.0 33.2 %copy-start.6 = (f32[2048]{0:T(1024)S(1)}, f32[2048]{0:T(1024)}, u32[]{:S(2)}) copy-start(f32[2048]{0:T(1024)} %param.27) | copy-start | bytes 24580
  137.0 51.6 %all-to-all-start.1 = ((bf16[1,32,144,256]{3,2,0,1:T(8,128)(2,1)}), bf16[1,32,144,256]{3,2,0,1:T(8,128)(2,1)}, u32[]{:S(2)}, u32[]{:S(2)}) async-start(bf16[1,32,144,256]{3,2,0,1:T(8,128)(2,1)} %bitcast.155), calls=%async_computation.2 | async-start | bytes 4718592 | tf_op jit(solution)/shard_map/all_to_all | solution.py:239
  169.4 0.8 copy-start.1
  321.9 5.9 %copy-start.5 = (f32[1,128,8]{1,2,0:T(8,128)S(1)}, f32[1,128,8]{1,2,0:T(8,128)}, u32[]{:S(2)}) copy-start(f32[1,128,8]{1,2,0:T(8,128)} %param.33) | copy-start | bytes 12292
  321.9 84.7 %all-to-all-start.3 = ((bf16[128,192,128]{2,1,0:T(8,128)(2,1)}), bf16[128,192,128]{2,1,0:T(8,128)(2,1)}, u32[]{:S(2)}, u32[]{:S(2)}) async-start(bf16[128,192,128]{2,1,0:T(8,128)(2,1)} %reshape_transpose_reshape.4), calls=%async_computation.4 | async-start | bytes 12582912 | tf_op jit(solution)/shard_map/all_to_all | solution.py:326
  417.8 3.5 copy-start.2
Sparse Core Ops, SparseCore 0:
  137.1 29.6 reduce-scatter.1

commit v3 on v2

--- a/solution.py
+++ b/solution.py
@@ -64,14 +64,14 @@
     def accumulate(masked):
         scores = lax.dot_general(
             q_ref[...], k_ref[...], (((1,), (1,)), ((), ())), preferred_element_type=jnp.float32
-        ) * scale
+        )
         if masked:
             visible = (qreq_ref[...] == kreq_ref[...]) & (kpos_ref[...] <= qpos_ref[...])
             scores = jnp.where(visible, scores, -jnp.inf)
         m_old = m_sc[...]
         m_new = jnp.maximum(m_old, jnp.max(scores, axis=1, keepdims=True))
-        expo = jnp.exp(scores - m_new)
-        factor = jnp.exp(m_old - m_new)
+        expo = jnp.exp((scores - m_new) * scale)
+        factor = jnp.exp((m_old - m_new) * scale)
         l_sc[...] = factor * l_sc[...] + jnp.sum(expo, axis=1, keepdims=True)
         acc_sc[...] = factor * acc_sc[...] + jnp.dot(
             expo.astype(jnp.bfloat16), v_ref[...], preferred_element_type=jnp.float32

time: 435 us -> 440 us (1.011)
  starting transfers between devices: 39.2 us -> 43.9 us
    all_to_all x1, starting transfers between devices: 24.3 us -> 28.9 us  [shards(): lax.all_to_all(outgoing_pages, 'seq', split_axis=1, concat_axis=1, tiled=...]
  transfers between devices with their start and end apart: 4 -> 4, of which waited for: 3 -> 3; matrix products, arithmetic and copies ran while one was open for 14% -> 13% of each run, Pallas kernels for 0% -> 0%
where the time goes in v3:
time: 440 us; the launch traced here: 438 us
  waiting for transfers between devices  115 us (26%)
  blocking collectives  84.4 us (19%)
  local copies, waits for them, and re-layouts  76.8 us (17%)
  matrix products  45.1 us (10%)
  starting transfers between devices  43.9 us (10%)
  Pallas kernels  29.9 us (7%)
  other arithmetic  27.9 us (6%)
  between operations  14.8 us (3%)
    all_to_all x1, blocking collectives, shards(): lax.all_to_all(outgoing, moe_axes, split_axis=0, concat_axis=0, tiled=True)  84.4 us
    all_to_all x1, waiting for transfers between devices, shards(): lax.all_to_all(done.reshape(device_count, exp_local * capacity * chunks,...  74.2 us
    all_to_all x1, waiting for transfers between devices, shards(): lax.all_to_all(jnp.broadcast_to(local_kv[None], (seq_size,) + local_kv.sh...  34.7 us
    pallas_call x1, Pallas kernels, flash_attention(): pl.pallas_call(functools.partial(flash_kernel, nkb, scale), grid_spec=gri...  29.9 us
    all_to_all x1, starting transfers between devices, shards(): lax.all_to_all(outgoing_pages, 'seq', split_axis=1, concat_axis=1, tiled=...  28.9 us
    dot_general x1, matrix products, expert_mlp(): jnp.einsum('erd,edf->erf', arrived, w_gate_up, preferred_element_type=jnp...  14.1 us
    gather x1, local copies, waits for them, and re-layouts, shards(): gathered = returned.reshape(experts * capacity, chunks, lanes)[target]  11.2 us
    another operation x1, local copies, waits for them, and re-layouts, shards(): done.reshape(device_count, exp_local * capacity * chunks, lanes)  10.5 us
  transfers between devices with their start and end apart: 4, of which 3 were waited for; matrix products, arithmetic and copies ran while one was open for 13% of the time, Pallas kernels for 0%

profile of v3, /device:TPU:25, one launch (start us, length us, event | category | flops | bytes accessed | tf_op | source)
XLA Modules:
  0.0 437.7 jit_solution(9168910683926247655)
XLA Ops:
  7.2 1.0 reduce-window.6
  8.2 0.7 fusion.69
  8.9 1.5 fusion.14
  10.4 0.8 copy.88
  11.2 0.8 copy.89
  12.1 2.0 convolution_convert_fusion.3
  14.0 2.0 multiply_reduce_fusion.1
  16.9 2.9 broadcast_in_dim.177
  19.8 9.0 %all-to-all-start = ((bf16[32,320,256]{2,1,0:T(8,128)(2,1)}), bf16[32,320,256]{2,1,0:T(8,128)(2,1)}, u32[]{:S(2)}, u32[]{:S(2)}) async-start(bf16[32,320,256]{2,1,0:T(8,128)(2,1)} %broadcast_in_dim.177), calls=%async_computation | async-start | bytes 10485760 | tf_op jit(solution)/shard_map/all_to_all | solution.py:199
  29.6 1.1 scatter_custom_fusion.1
  31.5 2.4 fusion
  34.0 1.3 copy.107
  35.3 1.4 copy.109
  36.7 6.5 %copy.105 = bf16[1024,2048]{1,0:T(8,128)(2,1)} copy(bf16[1024,2048]{0,1:T(8,128)(2,1)} %bitcast.158) | data formatting | bytes 8388608 | tf_op jit(solution)/shard_map/dot_general | solution.py:170
  43.3 3.9 multiply_reduce_fusion
  47.9 0.8 maximum_bitcast_fusion
  48.7 2.1 copy.84
  51.0 1.5 broadcast.447
  52.5 3.4 scatter_fusion
  56.0 3.2 pad_maximum_fusion.1
  59.8 34.7 %all-to-all-done = bf16[32,320,256]{2,1,0:T(8,128)(2,1)} async-done(((bf16[32,320,256]{2,1,0:T(8,128)(2,1)}), bf16[32,320,256]{2,1,0:T(8,128)(2,1)}, u32[]{:S(2)}, u32[]{:S(2)}) %all-to-all-start) | async-done | bytes 5242912 | tf_op jit(solution)/shard_map/all_to_all | solution.py:199
  94.5 1.3 slice.40
  95.8 2.5 slice.41
  98.2 5.4 %pad_maximum_fusion = (bf16[10240,128]{1,0:T(8,128)(2,1)}, bf16[10240,128]{1,0:T(8,128)(2,1)}) fusion(bf16[8192,256]{1,0:T(8,128)(2,1)S(1)} %bitcast.153, bf16[2048,256]{1,0:T(8,128)(2,1)S(1)} %bitcast.157), kind=kLoop, calls=%fused_computation.26 | loop fusion | flops 10485760 | bytes 10485760 | tf_op jit(solution)/shard_map/concatenate | solution.py:242
  103.6 29.9 %shard_map.194 = bf16[2048,128]{1,0:T(8,128)(2,1)} custom-call(s32[20]{0:T(128)} %select_select_fusion.live_ref, s32[2048,1]{1,0:T(8,128)} %bitcast.162, s32[2048,1]{1,0:T(8,128)} %bitcast.163, s32[1,10240]{1,0:T(1,128)} %bitcast.168, s32[1,10240]{1,0:T(1,128)} %bitcast.169, bf16[2048,128]{1,0:T(8,128)(2,1)} %bitcast.165, ...), custom_call_target="tpu_custom_call" | custom-call | flops 10737418240 | bytes 6291456 | tf_op jit(solution)/shard_map/pallas_call | solution.py:118
  133.5 2.0 copy.94
  135.6 4.6 %convolution_convert_fusion.2 = bf16[256,2048]{1,0:T(8,128)(2,1)} fusion(bf16[256,1024]{0,1:T(8,128)(2,1)} %bitcast.167, bf16[1024,2048]{1,0:T(8,128)(2,1)} %param.26), kind=kOutput, calls=%fused_computation.27 | convolution fusion | flops 1074266112 | bytes 5767168 | tf_op jit(solution)/shard_map/dot_general | solution.py:276
  140.2 28.9 %all-to-all-start.1 = ((bf16[1,32,144,256]{3,2,0,1:T(8,128)(2,1)}), bf16[1,32,144,256]{3,2,0,1:T(8,128)(2,1)}, u32[]{:S(2)}, u32[]{:S(2)}) async-start(bf16[1,32,144,256]{3,2,0,1:T(8,128)(2,1)} %bitcast.155), calls=%async_computation.2 | async-start | bytes 4718592 | tf_op jit(solution)/shard_map/all_to_all | solution.py:239
  170.1 5.6 %fusion.3 = pred[1536,128]{1,0:T(8,128)(4,1)S(1)} fusion(s32[128,8]{0,1:T(8,128)S(1)} %copy.97), kind=kLoop, calls=%fused_computation.11 | loop fusion | flops 2949120 | bytes 200704 | tf_op jit(solution)/shard_map/reduce_or | solution.py:309
  175.7 1.5 fusion.29
  177.2 0.8 copy-done.1
  178.0 4.5 %convolution_convert_fusion.1 = bf16[1536,2048]{1,0:T(8,128)(2,1)} fusion(pred[1536,128]{1,0:T(8,128)(4,1)S(1)} %fusion.3, bf16[128,2048]{1,0:T(8,128)(2,1)S(1)} %get-tuple-element.29, f32[2048]{0:T(1024)S(1)} %copy-done.6, f32[128]{0:T(128)S(1)} %add_rsqrt_fusion.3), kind=kOutput, calls=%fused_computation.8 | convolution fusion | flops 809500672 | bytes 7021056 | tf_op jit(solution)/shard_map/dot_general | solution.py:310
  182.5 10.4 %reshape.745 = bf16[128,192,128]{2,1,0:T(8,128)(2,1)} reshape(bf16[1536,2048]{1,0:T(8,128)(2,1)} %convolution_convert_fusion.1) | data formatting | bytes 12582912 | tf_op jit(solution)/shard_map/reshape | solution.py:311
  193.0 6.0 %all-to-all-done.1 = bf16[1,32,144,256]{3,2,0,1:T(8,128)(2,1)} async-done(((bf16[1,32,144,256]{3,2,0,1:T(8,128)(2,1)}), bf16[1,32,144,256]{3,2,0,1:T(8,128)(2,1)}, u32[]{:S(2)}, u32[]{:S(2)}) %all-to-all-start.1) | async-done | bytes 2359328 | tf_op jit(solution)/shard_map/all_to_all | solution.py:239
  198.9 1.5 fusion.60
  200.4 3.2 slice.60
  203.6 84.4 %all_to_all.20 = bf16[128,192,128]{2,1,0:T(8,128)(2,1)} all-to-all(bf16[128,192,128]{2,1,0:T(8,128)(2,1)} %reshape.745), channel_id=1, replica_groups=mesh['seq'=32,'tp'=2,'pd'=2] {'seq','tp','pd'}, dimensions={0} | all-to-all | bytes 12582912 | tf_op jit(solution)/shard_map/all_to_all | solution.py:315
  288.0 10.3 %reshape.746 = bf16[1536,2048]{1,0:T(8,128)(2,1)} reshape(bf16[128,192,128]{2,1,0:T(8,128)(2,1)} %all_to_all.20) | data formatting | bytes 12582912 | tf_op jit(solution)/shard_map/reshape.16
  298.3 14.1 %convolution_bitcast_fusion = f32[1,1536,1536]{2,1,0:T(8,128)S(1)} fusion(bf16[1536,2048]{1,0:T(8,128)(2,1)} %reshape.746, bf16[1,2048,1536]{2,1,0:T(8,128)(2,1)} %param.34), kind=kOutput, calls=%fused_computation.4 | convolution fusion | flops 9663676416 | bytes 22020096 | tf_op jit(solution)/shard_map/erd,edf->erf/dot_general | solution.py:130
  312.5 7.1 %convolution_convert_fusion = bf16[1536,2048]{1,0:T(8,128)(2,1)} fusion(bf16[1,768,2048]{2,1,0:T(8,128)(2,1)S(1)} %copy-done, f32[1,1536,1536]{2,1,0:T(8,128)S(1)} %convolution_bitcast_fusion), kind=kOutput, calls=%fused_computation.7 | convolution fusion | flops 4842061824 | bytes 18874368 | tf_op jit(solution)/shard_map/erf,efd->erd/dot_general | solution.py:133
  319.6 10.5 %reshape_transpose_reshape.4 = bf16[128,192,128]{2,1,0:T(8,128)(2,1)} reshape(bf16[1536,2048]{1,0:T(8,128)(2,1)} %convolution_convert_fusion) | data formatting | bytes 12582912 | tf_op jit(solution)/shard_map/reshape;transpose;reshape | solution.py:327
  330.0 5.9 %all-to-all-start.3 = ((bf16[128,192,128]{2,1,0:T(8,128)(2,1)}), bf16[128,192,128]{2,1,0:T(8,128)(2,1)}, u32[]{:S(2)}, u32[]{:S(2)}) async-start(bf16[128,192,128]{2,1,0:T(8,128)(2,1)} %reshape_transpose_reshape.4), calls=%async_computation.4 | async-start | bytes 12582912 | tf_op jit(solution)/shard_map/all_to_all | solution.py:326
  336.3 2.8 fusion.24
  339.1 1.3 copy.100
  340.5 74.2 %all-to-all-done.3 = bf16[128,192,128]{2,1,0:T(8,128)(2,1)} async-done(((bf16[128,192,128]{2,1,0:T(8,128)(2,1)}), bf16[128,192,128]{2,1,0:T(8,128)(2,1)}, u32[]{:S(2)}, u32[]{:S(2)}) %all-to-all-start.3) | async-done | bytes 6291488 | tf_op jit(solution)/shard_map/all_to_all | solution.py:326
  414.7 11.2 %gather_fusion = bf16[1024,16,128]{2,1,0:T(8,128)(2,1)} fusion(bf16[1536,16,128]{2,1,0:T(8,128)(2,1)} %bitcast.43, s32[1024]{0:T(1024)S(1)} %broadcast_clamp_fusion), kind=kCustom, calls=%fused_computation | custom fusion | bytes 8392704 | tf_op jit(solution)/shard_map/gather | solution.py:333
  426.0 3.5 fusion.5
  429.5 1.1 fusion.39
  (87 shorter events, 5.2 us)
Async XLA Ops:
  7.2 305.3 %copy-start = (bf16[1,768,2048]{2,1,0:T(8,128)(2,1)S(1)}, bf16[1,768,2048]{2,1,0:T(8,128)(2,1)}, u32[]{:S(2)}) copy-start(bf16[1,768,2048]{2,1,0:T(8,128)(2,1)} %param.35) | copy-start | bytes 9437188
  7.2 8.9 %copy-start.8 = (s32[1,8]{1,0:T(1,128)S(1)}, s32[1,8]{1,0:T(1,128)}, u32[]{:S(2)}) copy-start(s32[1,8]{1,0:T(1,128)} %param.31) | copy-start | bytes 100
  7.2 9.0 %copy-start.10 = (f32[128]{0:T(128)S(1)}, f32[128]{0:T(128)}, u32[]{:S(2)}) copy-start(f32[128]{0:T(128)} %param.25) | copy-start | bytes 1540
  19.8 9.1 %copy-start.9 = (s32[8,1,2,1]{0,3,2,1:T(1,128)S(1)}, s32[8,1,2,1]{0,3,2,1:T(1,128)}, u32[]{:S(2)}) copy-start(s32[8,1,2,1]{0,3,2,1:T(1,128)} %param.37) | copy-start | bytes 196
  19.8 74.7 %all-to-all-start = ((bf16[32,320,256]{2,1,0:T(8,128)(2,1)}), bf16[32,320,256]{2,1,0:T(8,128)(2,1)}, u32[]{:S(2)}, u32[]{:S(2)}) async-start(bf16[32,320,256]{2,1,0:T(8,128)(2,1)} %broadcast_in_dim.177), calls=%async_computation | async-start | bytes 10485760 | tf_op jit(solution)/shard_map/all_to_all | solution.py:199
  28.8 146.9 %reduce-scatter.2.cloned.1.call-start = ((), (), s32[]{:S(2)}) async-start(), calls=%async_computation.5 | async-start | bytes 1572864 | tf_op jit(solution)/shard_map/reduce_scatter | solution.py:275
  31.5 11.7 %copy-start.3 = (s32[10240]{0:T(1024)}, s32[10240]{0:T(1024)S(1)}, u32[]{:S(2)}) copy-start(s32[10240]{0:T(1024)S(1)} %get-tuple-element.46) | copy-start | bytes 122884
  31.5 11.7 %copy-start.4 = (s32[10240]{0:T(1024)}, s32[10240]{0:T(1024)S(1)}, u32[]{:S(2)}) copy-start(s32[10240]{0:T(1024)S(1)} %get-tuple-element.47) | copy-start | bytes 122884
  36.7 6.5 %copy-start.12 = (f32[2048]{0:T(1024)S(1)}, f32[2048]{0:T(1024)}, u32[]{:S(2)}) copy-start(f32[2048]{0:T(1024)} %param.20) | copy-start | bytes 24580
  43.2 4.2 copy-start.11
  140.2 28.9 %copy-start.7 = (s32[1,128,8]{1,2,0:T(8,128)S(1)}, s32[1,128,8]{1,2,0:T(8,128)}, u32[]{:S(2)}) copy-start(s32[1,128,8]{1,2,0:T(8,128)} %param.32) | copy-start | bytes 12292
  140.2 37.8 %copy-start.6 = (f32[2048]{0:T(1024)S(1)}, f32[2048]{0:T(1024)}, u32[]{:S(2)}) copy-start(f32[2048]{0:T(1024)} %param.27) | copy-start | bytes 24580
  140.2 58.7 %all-to-all-start.1 = ((bf16[1,32,144,256]{3,2,0,1:T(8,128)(2,1)}), bf16[1,32,144,256]{3,2,0,1:T(8,128)(2,1)}, u32[]{:S(2)}, u32[]{:S(2)}) async-start(bf16[1,32,144,256]{3,2,0,1:T(8,128)(2,1)} %bitcast.155), calls=%async_computation.2 | async-start | bytes 4718592 | tf_op jit(solution)/shard_map/all_to_all | solution.py:239
  177.2 0.8 copy-start.1
  330.0 6.0 %copy-start.5 = (f32[1,128,8]{1,2,0:T(8,128)S(1)}, f32[1,128,8]{1,2,0:T(8,128)}, u32[]{:S(2)}) copy-start(f32[1,128,8]{1,2,0:T(8,128)} %param.33) | copy-start | bytes 12292
  330.0 84.7 %all-to-all-start.3 = ((bf16[128,192,128]{2,1,0:T(8,128)(2,1)}), bf16[128,192,128]{2,1,0:T(8,128)(2,1)}, u32[]{:S(2)}, u32[]{:S(2)}) async-start(bf16[128,192,128]{2,1,0:T(8,128)(2,1)} %reshape_transpose_reshape.4), calls=%async_computation.4 | async-start | bytes 12582912 | tf_op jit(solution)/shard_map/all_to_all | solution.py:326
  426.0 3.5 copy-start.2
Sparse Core Ops, SparseCore 0:
  140.3 34.0 reduce-scatter.1

commit v4 on v3

--- a/solution.py
+++ b/solution.py
@@ -309,9 +309,6 @@
     placing_rows = jnp.any(slot_of, axis=2).astype(jnp.bfloat16)
     outgoing = jnp.dot(placing_rows, mixed, preferred_element_type=jnp.float32).astype(jnp.bfloat16)
     outgoing = outgoing.reshape(device_count, exp_local * capacity * chunks, lanes)
-    outgoing, arrived_pages, arrived_slots = lax.optimization_barrier(
-        (outgoing, arrived_pages, arrived_slots)
-    )
     arrived = lax.all_to_all(outgoing, moe_axes, split_axis=0, concat_axis=0, tiled=True)
     expert_rows = (
         arrived.reshape(device_count, exp_local, capacity, width)

time: 440 us -> 432 us (0.982)
  starting transfers between devices: 43.9 us -> 23.6 us
  waiting for transfers between devices: 115 us -> 135 us
  Pallas kernels: 29.9 us -> 24.3 us
    reduce_scatter x1, waiting for transfers between devices: 0.02 us -> 28.1 us  [shards(): lax.psum_scatter(jnp.dot(attn, w_out, preferred_element_type=jnp.float32)...]
    all_to_all x1, starting transfers between devices: 28.9 us -> 4.6 us  [shards(): lax.all_to_all(outgoing_pages, 'seq', split_axis=1, concat_axis=1, tiled=...]
    all_to_all x1, waiting for transfers between devices: 5.97 us -> 0.01 us  [shards(): lax.all_to_all(outgoing_pages, 'seq', split_axis=1, concat_axis=1, tiled=...]
    pallas_call x1, Pallas kernels: 29.9 us -> 24.3 us  [flash_attention(): pl.pallas_call(functools.partial(flash_kernel, nkb, scale), grid_spec=gri...]
  transfers between devices with their start and end apart: 4 -> 4, of which waited for: 3 -> 3; matrix products, arithmetic and copies ran while one was open for 13% -> 20% of each run, Pallas kernels for 0% -> 0%
where the time goes in v4:
time: 432 us; the launch traced here: 429 us
  waiting for transfers between devices  135 us (31%)
  blocking collectives  84.9 us (20%)
  local copies, waits for them, and re-layouts  75.3 us (17%)
  matrix products  43.4 us (10%)
  other arithmetic  28.1 us (7%)
  Pallas kernels  24.3 us (6%)
  starting transfers between devices  23.6 us (5%)
  between operations  14.8 us (3%)
    all_to_all x1, blocking collectives, shards(): lax.all_to_all(outgoing, moe_axes, split_axis=0, concat_axis=0, tiled=True)  84.9 us
    all_to_all x1, waiting for transfers between devices, shards(): lax.all_to_all(done.reshape(device_count, exp_local * capacity * chunks,...  71.8 us
    all_to_all x1, waiting for transfers between devices, shards(): lax.all_to_all(jnp.broadcast_to(local_kv[None], (seq_size,) + local_kv.sh...  34.6 us
    reduce_scatter x1, waiting for transfers between devices, shards(): lax.psum_scatter(jnp.dot(attn, w_out, preferred_element_type=jnp.float32)...  28.1 us
    pallas_call x1, Pallas kernels, flash_attention(): pl.pallas_call(functools.partial(flash_kernel, nkb, scale), grid_spec=gri...  24.3 us
    dot_general x1, matrix products, expert_mlp(): jnp.einsum('erd,edf->erf', arrived, w_gate_up, preferred_element_type=jnp...  14.1 us
    gather x1, local copies, waits for them, and re-layouts, shards(): gathered = returned.reshape(experts * capacity, chunks, lanes)[target]  11.2 us
    reshape x1, local copies, waits for them, and re-layouts, shards(): outgoing.reshape(device_count, exp_local * capacity * chunks, lanes)  10.5 us
  transfers between devices with their start and end apart: 4, of which 3 were waited for; matrix products, arithmetic and copies ran while one was open for 20% of the time, Pallas kernels for 0%

profile of v4, /device:TPU:25, one launch (start us, length us, event | category | flops | bytes accessed | tf_op | source)
XLA Modules:
  0.0 429.0 jit_solution(12234094847572049536)
XLA Ops:
  7.2 1.0 reduce-window.6
  8.2 0.7 fusion.64
  8.9 1.5 fusion.14
  10.4 0.8 copy.70
  11.2 0.8 copy.71
  12.1 2.0 convolution_convert_fusion.3
  14.0 2.0 multiply_reduce_fusion.1
  16.9 2.9 broadcast_in_dim.177
  19.8 9.0 %all-to-all-start = ((bf16[32,320,256]{2,1,0:T(8,128)(2,1)}), bf16[32,320,256]{2,1,0:T(8,128)(2,1)}, u32[]{:S(2)}, u32[]{:S(2)}) async-start(bf16[32,320,256]{2,1,0:T(8,128)(2,1)} %broadcast_in_dim.177), calls=%async_computation | async-start | bytes 10485760 | tf_op jit(solution)/shard_map/all_to_all | solution.py:199
  29.6 1.1 scatter_custom_fusion.1
  31.5 2.4 fusion
  34.0 1.3 copy.90
  35.3 1.4 copy.92
  36.7 6.5 %copy.87 = bf16[1024,2048]{1,0:T(8,128)(2,1)} copy(bf16[1024,2048]{0,1:T(8,128)(2,1)} %bitcast.161) | data formatting | bytes 8388608 | tf_op jit(solution)/shard_map/dot_general | solution.py:170
  43.3 3.9 multiply_reduce_fusion
  47.9 0.8 maximum_bitcast_fusion
  48.7 2.1 copy.66
  51.0 1.5 broadcast.447
  52.5 3.4 scatter_fusion
  56.0 3.2 pad_maximum_fusion.1
  59.8 34.6 %all-to-all-done = bf16[32,320,256]{2,1,0:T(8,128)(2,1)} async-done(((bf16[32,320,256]{2,1,0:T(8,128)(2,1)}), bf16[32,320,256]{2,1,0:T(8,128)(2,1)}, u32[]{:S(2)}, u32[]{:S(2)}) %all-to-all-start) | async-done | bytes 5242912 | tf_op jit(solution)/shard_map/all_to_all | solution.py:199
  94.5 1.3 slice.40
  95.8 2.5 slice.41
  98.2 5.4 %pad_maximum_fusion = (bf16[10240,128]{1,0:T(8,128)(2,1)}, bf16[10240,128]{1,0:T(8,128)(2,1)}) fusion(bf16[8192,256]{1,0:T(8,128)(2,1)S(1)} %bitcast.157, bf16[2048,256]{1,0:T(8,128)(2,1)S(1)} %bitcast.160), kind=kLoop, calls=%fused_computation.26 | loop fusion | flops 10485760 | bytes 10485760 | tf_op jit(solution)/shard_map/concatenate | solution.py:242
  103.6 24.3 %shard_map.194 = bf16[2048,128]{1,0:T(8,128)(2,1)} custom-call(s32[20]{0:T(128)} %select_select_fusion.live_ref, s32[2048,1]{1,0:T(8,128)} %bitcast.165, s32[2048,1]{1,0:T(8,128)} %bitcast.166, s32[1,10240]{1,0:T(1,128)} %bitcast.171, s32[1,10240]{1,0:T(1,128)} %bitcast.172, bf16[2048,128]{1,0:T(8,128)(2,1)} %bitcast.168, ...), custom_call_target="tpu_custom_call" | custom-call | flops 10737418240 | bytes 6291456 | tf_op jit(solution)/shard_map/pallas_call | solution.py:118
  127.9 2.0 copy.76
  129.9 4.6 %convolution_convert_fusion.2 = bf16[256,2048]{1,0:T(8,128)(2,1)} fusion(bf16[256,1024]{0,1:T(8,128)(2,1)} %bitcast.170, bf16[1024,2048]{1,0:T(8,128)(2,1)} %param.26), kind=kOutput, calls=%fused_computation.27 | convolution fusion | flops 1074266112 | bytes 5767168 | tf_op jit(solution)/shard_map/dot_general | solution.py:276
  135.6 5.8 %fusion.3 = pred[1536,128]{1,0:T(8,128)(4,1)S(1)} fusion(s32[128,8]{0,1:T(8,128)S(1)} %copy.79), kind=kLoop, calls=%fused_computation.11 | loop fusion | flops 2949120 | bytes 200704 | tf_op jit(solution)/shard_map/reduce_or | solution.py:309
  141.4 28.1 %reduce-scatter.2.cloned.1.call-done = bf16[128,2048]{1,0:T(8,128)(2,1)} async-done(((bf16[256,2048]{1,0:T(8,128)(2,1)}), bf16[128,2048]{1,0:T(8,128)(2,1)}) %reduce-scatter.2.cloned.1.call-update) | async-done | bytes 524304 | tf_op jit(solution)/shard_map/reduce_scatter | solution.py:275
  169.5 1.5 fusion.24
  171.0 0.8 copy-done.1
  171.7 4.5 %convolution_convert_fusion.1 = bf16[1536,2048]{1,0:T(8,128)(2,1)} fusion(pred[1536,128]{1,0:T(8,128)(4,1)S(1)} %fusion.3, bf16[128,2048]{1,0:T(8,128)(2,1)S(1)} %get-tuple-element.21, f32[2048]{0:T(1024)S(1)} %copy-done.6, f32[128]{0:T(128)S(1)} %add_rsqrt_fusion.3), kind=kOutput, calls=%fused_computation.8 | convolution fusion | flops 809500672 | bytes 7021056 | tf_op jit(solution)/shard_map/dot_general | solution.py:310
  176.3 10.5 %reshape.740 = bf16[128,192,128]{2,1,0:T(8,128)(2,1)} reshape(bf16[1536,2048]{1,0:T(8,128)(2,1)} %convolution_convert_fusion.1) | data formatting | bytes 12582912 | tf_op jit(solution)/shard_map/reshape | solution.py:311
  186.7 84.9 %all_to_all.20 = bf16[128,192,128]{2,1,0:T(8,128)(2,1)} all-to-all(bf16[128,192,128]{2,1,0:T(8,128)(2,1)} %reshape.740), channel_id=1, replica_groups=mesh['seq'=32,'tp'=2,'pd'=2] {'seq','tp','pd'}, dimensions={0} | all-to-all | bytes 12582912 | tf_op jit(solution)/shard_map/all_to_all | solution.py:312
  271.6 4.6 %all-to-all-start.3 = ((bf16[1,32,144,256]{3,2,0,1:T(8,128)(2,1)}), bf16[1,32,144,256]{3,2,0,1:T(8,128)(2,1)}, u32[]{:S(2)}, u32[]{:S(2)}) async-start(bf16[1,32,144,256]{3,2,0,1:T(8,128)(2,1)} %bitcast.159), calls=%async_computation.4 | async-start | bytes 4718592 | tf_op jit(solution)/shard_map/all_to_all | solution.py:239
  276.2 10.3 %reshape.741 = bf16[1536,2048]{1,0:T(8,128)(2,1)} reshape(bf16[128,192,128]{2,1,0:T(8,128)(2,1)} %all_to_all.20) | data formatting | bytes 12582912 | tf_op jit(solution)/shard_map/reshape.16
  286.6 14.1 %convolution_bitcast_fusion = f32[1,1536,1536]{2,1,0:T(8,128)S(1)} fusion(bf16[1536,2048]{1,0:T(8,128)(2,1)} %reshape.741, bf16[1,2048,1536]{2,1,0:T(8,128)(2,1)} %param.34), kind=kOutput, calls=%fused_computation.4 | convolution fusion | flops 9663676416 | bytes 22020096 | tf_op jit(solution)/shard_map/erd,edf->erf/dot_general | solution.py:130
  300.7 7.0 %convolution_convert_fusion = bf16[1536,2048]{1,0:T(8,128)(2,1)} fusion(bf16[1,768,2048]{2,1,0:T(8,128)(2,1)S(1)} %copy-done, f32[1,1536,1536]{2,1,0:T(8,128)S(1)} %convolution_bitcast_fusion), kind=kOutput, calls=%fused_computation.7 | convolution fusion | flops 4842061824 | bytes 18874368 | tf_op jit(solution)/shard_map/erf,efd->erd/dot_general | solution.py:133
  307.7 10.4 %reshape_transpose_reshape.4 = bf16[128,192,128]{2,1,0:T(8,128)(2,1)} reshape(bf16[1536,2048]{1,0:T(8,128)(2,1)} %convolution_convert_fusion) | data formatting | bytes 12582912 | tf_op jit(solution)/shard_map/reshape;transpose;reshape | solution.py:324
  318.2 9.9 %all-to-all-start.2 = ((bf16[128,192,128]{2,1,0:T(8,128)(2,1)}), bf16[128,192,128]{2,1,0:T(8,128)(2,1)}, u32[]{:S(2)}, u32[]{:S(2)}) async-start(bf16[128,192,128]{2,1,0:T(8,128)(2,1)} %reshape_transpose_reshape.4), calls=%async_computation.3 | async-start | bytes 12582912 | tf_op jit(solution)/shard_map/all_to_all | solution.py:323
  328.4 1.7 slice.63
  330.2 1.5 fusion.55
  331.7 1.3 fusion.21
  332.9 1.3 copy.82
  334.3 71.8 %all-to-all-done.2 = bf16[128,192,128]{2,1,0:T(8,128)(2,1)} async-done(((bf16[128,192,128]{2,1,0:T(8,128)(2,1)}), bf16[128,192,128]{2,1,0:T(8,128)(2,1)}, u32[]{:S(2)}, u32[]{:S(2)}) %all-to-all-start.2) | async-done | bytes 6291488 | tf_op jit(solution)/shard_map/all_to_all | solution.py:323
  406.1 11.2 %gather_fusion = bf16[1024,16,128]{2,1,0:T(8,128)(2,1)} fusion(bf16[1536,16,128]{2,1,0:T(8,128)(2,1)} %bitcast.42, s32[1024]{0:T(1024)S(1)} %broadcast_clamp_fusion), kind=kCustom, calls=%fused_computation | custom fusion | bytes 8392704 | tf_op jit(solution)/shard_map/gather | solution.py:330
  417.2 3.5 fusion.5
  420.7 1.1 fusion.34
  (87 shorter events, 5.2 us)
Async XLA Ops:
  7.2 293.6 %copy-start = (bf16[1,768,2048]{2,1,0:T(8,128)(2,1)S(1)}, bf16[1,768,2048]{2,1,0:T(8,128)(2,1)}, u32[]{:S(2)}) copy-start(bf16[1,768,2048]{2,1,0:T(8,128)(2,1)} %param.35) | copy-start | bytes 9437188
  7.2 8.9 %copy-start.8 = (s32[1,8]{1,0:T(1,128)S(1)}, s32[1,8]{1,0:T(1,128)}, u32[]{:S(2)}) copy-start(s32[1,8]{1,0:T(1,128)} %param.31) | copy-start | bytes 100
  7.2 9.0 %copy-start.10 = (f32[128]{0:T(128)S(1)}, f32[128]{0:T(128)}, u32[]{:S(2)}) copy-start(f32[128]{0:T(128)} %param.25) | copy-start | bytes 1540
  19.8 9.1 %copy-start.9 = (s32[8,1,2,1]{0,3,2,1:T(1,128)S(1)}, s32[8,1,2,1]{0,3,2,1:T(1,128)}, u32[]{:S(2)}) copy-start(s32[8,1,2,1]{0,3,2,1:T(1,128)} %param.37) | copy-start | bytes 196
  19.8 74.7 %all-to-all-start = ((bf16[32,320,256]{2,1,0:T(8,128)(2,1)}), bf16[32,320,256]{2,1,0:T(8,128)(2,1)}, u32[]{:S(2)}, u32[]{:S(2)}) async-start(bf16[32,320,256]{2,1,0:T(8,128)(2,1)} %broadcast_in_dim.177), calls=%async_computation | async-start | bytes 10485760 | tf_op jit(solution)/shard_map/all_to_all | solution.py:199
  28.8 140.6 %reduce-scatter.2.cloned.1.call-start = ((), (), s32[]{:S(2)}) async-start(), calls=%async_computation.5 | async-start | bytes 1572864 | tf_op jit(solution)/shard_map/reduce_scatter | solution.py:275
  31.5 11.7 %copy-start.3 = (s32[10240]{0:T(1024)}, s32[10240]{0:T(1024)S(1)}, u32[]{:S(2)}) copy-start(s32[10240]{0:T(1024)S(1)} %get-tuple-element.38) | copy-start | bytes 122884
  31.5 11.7 %copy-start.4 = (s32[10240]{0:T(1024)}, s32[10240]{0:T(1024)S(1)}, u32[]{:S(2)}) copy-start(s32[10240]{0:T(1024)S(1)} %get-tuple-element.39) | copy-start | bytes 122884
  36.7 6.5 %copy-start.12 = (f32[2048]{0:T(1024)S(1)}, f32[2048]{0:T(1024)}, u32[]{:S(2)}) copy-start(f32[2048]{0:T(1024)} %param.20) | copy-start | bytes 24580
  43.2 4.2 copy-start.11
  129.9 4.6 %copy-start.7 = (s32[1,128,8]{1,2,0:T(8,128)S(1)}, s32[1,128,8]{1,2,0:T(8,128)}, u32[]{:S(2)}) copy-start(s32[1,128,8]{1,2,0:T(8,128)} %param.32) | copy-start | bytes 12292
  134.5 37.2 %copy-start.6 = (f32[2048]{0:T(1024)S(1)}, f32[2048]{0:T(1024)}, u32[]{:S(2)}) copy-start(f32[2048]{0:T(1024)} %param.27) | copy-start | bytes 24580
  170.9 0.8 copy-start.1
  271.6 46.5 %all-to-all-start.3 = ((bf16[1,32,144,256]{3,2,0,1:T(8,128)(2,1)}), bf16[1,32,144,256]{3,2,0,1:T(8,128)(2,1)}, u32[]{:S(2)}, u32[]{:S(2)}) async-start(bf16[1,32,144,256]{3,2,0,1:T(8,128)(2,1)} %bitcast.159), calls=%async_computation.4 | async-start | bytes 4718592 | tf_op jit(solution)/shard_map/all_to_all | solution.py:239
  318.2 10.0 %copy-start.5 = (f32[1,128,8]{1,2,0:T(8,128)S(1)}, f32[1,128,8]{1,2,0:T(8,128)}, u32[]{:S(2)}) copy-start(f32[1,128,8]{1,2,0:T(8,128)} %param.33) | copy-start | bytes 12292
  318.2 87.9 %all-to-all-start.2 = ((bf16[128,192,128]{2,1,0:T(8,128)(2,1)}), bf16[128,192,128]{2,1,0:T(8,128)(2,1)}, u32[]{:S(2)}, u32[]{:S(2)}) async-start(bf16[128,192,128]{2,1,0:T(8,128)(2,1)} %reshape_transpose_reshape.4), calls=%async_computation.3 | async-start | bytes 12582912 | tf_op jit(solution)/shard_map/all_to_all | solution.py:323
  417.2 3.5 copy-start.2
Sparse Core Ops, SparseCore 0:
  134.7 34.7 reduce-scatter.1

commit v5 on v3

--- a/solution.py
+++ b/solution.py
@@ -307,7 +307,9 @@
         == jnp.arange(experts * capacity, dtype=jnp.int32)[:, None, None]
     )
     placing_rows = jnp.any(slot_of, axis=2).astype(jnp.bfloat16)
-    outgoing = jnp.dot(placing_rows, mixed, preferred_element_type=jnp.float32).astype(jnp.bfloat16)
+    outgoing = jnp.einsum(
+        "st,tcl->scl", placing_rows, mixed.reshape(half, chunks, lanes), preferred_element_type=jnp.float32
+    ).astype(jnp.bfloat16)
     outgoing = outgoing.reshape(device_count, exp_local * capacity * chunks, lanes)
     outgoing, arrived_pages, arrived_slots = lax.optimization_barrier(
         (outgoing, arrived_pages, arrived_slots)

time: 440 us -> 439 us (level)
  waiting for transfers between devices: 115 us -> 108 us
  local copies, waits for them, and re-layouts: 76.8 us -> 83.7 us
  Pallas kernels: 29.9 us -> 23.3 us
    convert_element_type x0 -> x1, local copies, waits for them, and re-layouts: none -> 18.4 us  [shards(): outgoing = jnp.einsum('st,tcl->scl', placing_rows, mixed.reshape(half, ch...]
    reshape x1 -> x0, local copies, waits for them, and re-layouts: 10.4 us -> none  [shards(): outgoing.reshape(device_count, exp_local * capacity * chunks, lanes)]
    pallas_call x1, Pallas kernels: 29.9 us -> 23.3 us  [flash_attention(): pl.pallas_call(functools.partial(flash_kernel, nkb, scale), grid_spec=gri...]
    all_to_all x1, waiting for transfers between devices: 5.97 us -> 0.01 us  [shards(): lax.all_to_all(outgoing_pages, 'seq', split_axis=1, concat_axis=1, tiled=...]
  transfers between devices with their start and end apart: 4 -> 4, of which waited for: 3 -> 2; matrix products, arithmetic and copies ran while one was open for 13% -> 15% of each run, Pallas kernels for 0% -> 0%
where the time goes in v5:
time: 439 us; the launch traced here: 433 us
  waiting for transfers between devices  108 us (25%)
  blocking collectives  86.6 us (20%)
  local copies, waits for them, and re-layouts  83.7 us (19%)
  starting transfers between devices  45.5 us (10%)
  matrix products  42.4 us (10%)
  other arithmetic  27.9 us (6%)
  Pallas kernels  23.3 us (5%)
  between operations  14.8 us (3%)
    all_to_all x1, blocking collectives, shards(): lax.all_to_all(outgoing, moe_axes, split_axis=0, concat_axis=0, tiled=True)  86.6 us
    all_to_all x1, waiting for transfers between devices, shards(): lax.all_to_all(done.reshape(device_count, exp_local * capacity * chunks,...  73.5 us
    all_to_all x1, waiting for transfers between devices, shards(): lax.all_to_all(jnp.broadcast_to(local_kv[None], (seq_size,) + local_kv.sh...  34.9 us
    all_to_all x1, starting transfers between devices, shards(): lax.all_to_all(outgoing_pages, 'seq', split_axis=1, concat_axis=1, tiled=...  30.1 us
    pallas_call x1, Pallas kernels, flash_attention(): pl.pallas_call(functools.partial(flash_kernel, nkb, scale), grid_spec=gri...  23.3 us
    convert_element_type x1, local copies, waits for them, and re-layouts, shards(): outgoing = jnp.einsum('st,tcl->scl', placing_rows, mixed.reshape(half, ch...  18.4 us
    dot_general x1, matrix products, expert_mlp(): jnp.einsum('erd,edf->erf', arrived, w_gate_up, preferred_element_type=jnp...  14.1 us
    gather x1, local copies, waits for them, and re-layouts, shards(): gathered = returned.reshape(experts * capacity, chunks, lanes)[target]  11.2 us
  transfers between devices with their start and end apart: 4, of which 2 were waited for; matrix products, arithmetic and copies ran while one was open for 15% of the time, Pallas kernels for 0%

profile of v5, /device:TPU:25, one launch (start us, length us, event | category | flops | bytes accessed | tf_op | source)
XLA Modules:
  0.0 432.6 jit_solution(126754692578934133)
XLA Ops:
  7.2 1.0 reduce-window.6
  8.2 0.7 fusion.70
  8.9 1.5 fusion.14
  10.4 0.8 copy.95
  11.2 0.8 copy.96
  12.1 2.0 convolution_convert_fusion.3
  14.0 2.0 multiply_reduce_fusion.1
  16.9 2.9 broadcast_in_dim.177
  19.8 9.0 %all-to-all-start = ((bf16[32,320,256]{2,1,0:T(8,128)(2,1)}), bf16[32,320,256]{2,1,0:T(8,128)(2,1)}, u32[]{:S(2)}, u32[]{:S(2)}) async-start(bf16[32,320,256]{2,1,0:T(8,128)(2,1)} %broadcast_in_dim.177), calls=%async_computation | async-start | bytes 10485760 | tf_op jit(solution)/shard_map/all_to_all | solution.py:199
  29.6 0.8 scatter_custom_fusion.1
  31.1 2.4 fusion
  33.6 1.3 copy.117
  35.0 1.4 copy.119
  36.3 6.5 %copy.114 = bf16[1024,2048]{1,0:T(8,128)(2,1)} copy(bf16[1024,2048]{0,1:T(8,128)(2,1)} %bitcast.169) | data formatting | bytes 8388608 | tf_op jit(solution)/shard_map/dot_general | solution.py:170
  42.9 3.9 multiply_reduce_fusion
  47.5 0.8 maximum_bitcast_fusion
  48.3 2.1 copy.91
  50.6 1.6 broadcast.447
  52.2 3.4 scatter_fusion
  55.7 3.2 pad_maximum_fusion.1
  58.9 0.6 select_select_fusion.live_ref
  59.5 34.9 %all-to-all-done = bf16[32,320,256]{2,1,0:T(8,128)(2,1)} async-done(((bf16[32,320,256]{2,1,0:T(8,128)(2,1)}), bf16[32,320,256]{2,1,0:T(8,128)(2,1)}, u32[]{:S(2)}, u32[]{:S(2)}) %all-to-all-start) | async-done | bytes 5242912 | tf_op jit(solution)/shard_map/all_to_all | solution.py:199
  94.4 1.3 slice.40
  95.7 2.5 slice.41
  98.1 5.4 %pad_maximum_fusion = (bf16[10240,128]{1,0:T(8,128)(2,1)}, bf16[10240,128]{1,0:T(8,128)(2,1)}) fusion(bf16[8192,256]{1,0:T(8,128)(2,1)S(1)} %bitcast.164, bf16[2048,256]{1,0:T(8,128)(2,1)S(1)} %bitcast.168), kind=kLoop, calls=%fused_computation.26 | loop fusion | flops 10485760 | bytes 10485760 | tf_op jit(solution)/shard_map/concatenate | solution.py:242
  103.5 23.3 %shard_map.194 = bf16[2048,128]{1,0:T(8,128)(2,1)} custom-call(s32[20]{0:T(128)} %select_select_fusion.live_ref, s32[2048,1]{1,0:T(8,128)} %bitcast.173, s32[2048,1]{1,0:T(8,128)} %bitcast.174, s32[1,10240]{1,0:T(1,128)} %bitcast.179, s32[1,10240]{1,0:T(1,128)} %bitcast.180, bf16[2048,128]{1,0:T(8,128)(2,1)} %bitcast.176, ...), custom_call_target="tpu_custom_call" | custom-call | flops 10737418240 | bytes 6291456 | tf_op jit(solution)/shard_map/pallas_call | solution.py:118
  126.8 2.0 copy.101
  128.8 4.6 %convolution_convert_fusion.2 = bf16[256,2048]{1,0:T(8,128)(2,1)} fusion(bf16[256,1024]{0,1:T(8,128)(2,1)} %bitcast.178, bf16[1024,2048]{1,0:T(8,128)(2,1)} %param.26), kind=kOutput, calls=%fused_computation.27 | convolution fusion | flops 1074266112 | bytes 5767168 | tf_op jit(solution)/shard_map/dot_general | solution.py:276
  133.5 30.1 %all-to-all-start.1 = ((bf16[1,32,144,256]{3,2,0,1:T(8,128)(2,1)}), bf16[1,32,144,256]{3,2,0,1:T(8,128)(2,1)}, u32[]{:S(2)}, u32[]{:S(2)}) async-start(bf16[1,32,144,256]{3,2,0,1:T(8,128)(2,1)} %bitcast.166), calls=%async_computation.2 | async-start | bytes 4718592 | tf_op jit(solution)/shard_map/all_to_all | solution.py:239
  163.8 0.6 fusion.28
  164.6 5.6 %fusion.3 = pred[1536,128]{1,0:T(8,128)(4,1)S(1)} fusion(s32[128,8]{0,1:T(8,128)S(1)} %copy.104), kind=kLoop, calls=%fused_computation.10 | loop fusion | flops 2949120 | bytes 200704 | tf_op jit(solution)/shard_map/reduce_or | solution.py:309
  170.2 1.5 fusion.29
  171.7 1.9 convolution_convert_fusion.1
  173.6 18.4 %copy.106 = bf16[1536,16,128]{2,1,0:T(8,128)(2,1)} copy(bf16[1536,16,128]{2,0,1:T(8,128)(2,1)S(1)} %convolution_convert_fusion.1) | data formatting | bytes 12582912 | tf_op jit(solution)/shard_map/convert_element_type | solution.py:312
  192.0 1.5 fusion.61
  193.5 3.2 slice.60
  196.7 86.6 %all_to_all.20 = bf16[128,192,128]{2,1,0:T(8,128)(2,1)} all-to-all(bf16[128,192,128]{2,1,0:T(8,128)(2,1)} %bitcast.163), channel_id=1, replica_groups=mesh['seq'=32,'tp'=2,'pd'=2] {'seq','tp','pd'}, dimensions={0} | all-to-all | bytes 12582912 | tf_op jit(solution)/shard_map/all_to_all | solution.py:317
  283.3 10.3 %reshape.750 = bf16[1536,2048]{1,0:T(8,128)(2,1)} reshape(bf16[128,192,128]{2,1,0:T(8,128)(2,1)} %all_to_all.20) | data formatting | bytes 12582912 | tf_op jit(solution)/shard_map/reshape.16
  293.6 14.1 %convolution_bitcast_fusion = f32[1,1536,1536]{2,1,0:T(8,128)S(1)} fusion(bf16[1536,2048]{1,0:T(8,128)(2,1)} %reshape.750, bf16[1,2048,1536]{2,1,0:T(8,128)(2,1)} %param.34), kind=kOutput, calls=%fused_computation.4 | convolution fusion | flops 9663676416 | bytes 22020096 | tf_op jit(solution)/shard_map/erd,edf->erf/dot_general | solution.py:130
  307.8 7.1 %convolution_convert_fusion = bf16[1536,2048]{1,0:T(8,128)(2,1)} fusion(bf16[1,768,2048]{2,1,0:T(8,128)(2,1)S(1)} %copy-done, f32[1,1536,1536]{2,1,0:T(8,128)S(1)} %convolution_bitcast_fusion), kind=kOutput, calls=%fused_computation.7 | convolution fusion | flops 4842061824 | bytes 18874368 | tf_op jit(solution)/shard_map/erf,efd->erd/dot_general | solution.py:133
  314.8 10.5 %reshape_transpose_reshape.4 = bf16[128,192,128]{2,1,0:T(8,128)(2,1)} reshape(bf16[1536,2048]{1,0:T(8,128)(2,1)} %convolution_convert_fusion) | data formatting | bytes 12582912 | tf_op jit(solution)/shard_map/reshape;transpose;reshape | solution.py:329
  325.3 6.4 %all-to-all-start.3 = ((bf16[128,192,128]{2,1,0:T(8,128)(2,1)}), bf16[128,192,128]{2,1,0:T(8,128)(2,1)}, u32[]{:S(2)}, u32[]{:S(2)}) async-start(bf16[128,192,128]{2,1,0:T(8,128)(2,1)} %reshape_transpose_reshape.4), calls=%async_computation.4 | async-start | bytes 12582912 | tf_op jit(solution)/shard_map/all_to_all | solution.py:328
  332.0 2.8 fusion.24
  334.8 1.3 copy.109
  336.1 73.5 %all-to-all-done.3 = bf16[128,192,128]{2,1,0:T(8,128)(2,1)} async-done(((bf16[128,192,128]{2,1,0:T(8,128)(2,1)}), bf16[128,192,128]{2,1,0:T(8,128)(2,1)}, u32[]{:S(2)}, u32[]{:S(2)}) %all-to-all-start.3) | async-done | bytes 6291488 | tf_op jit(solution)/shard_map/all_to_all | solution.py:328
  409.6 11.2 %gather_fusion = bf16[1024,16,128]{2,1,0:T(8,128)(2,1)} fusion(bf16[1536,16,128]{2,1,0:T(8,128)(2,1)} %bitcast.45, s32[1024]{0:T(1024)S(1)} %broadcast_clamp_fusion), kind=kCustom, calls=%fused_computation | custom fusion | bytes 8392704 | tf_op jit(solution)/shard_map/gather | solution.py:335
  420.9 3.5 fusion.5
  424.4 1.1 fusion.40
  (87 shorter events, 4.0 us)
Async XLA Ops:
  7.2 300.6 %copy-start = (bf16[1,768,2048]{2,1,0:T(8,128)(2,1)S(1)}, bf16[1,768,2048]{2,1,0:T(8,128)(2,1)}, u32[]{:S(2)}) copy-start(bf16[1,768,2048]{2,1,0:T(8,128)(2,1)} %param.35) | copy-start | bytes 9437188
  7.2 8.9 %copy-start.8 = (s32[1,8]{1,0:T(1,128)S(1)}, s32[1,8]{1,0:T(1,128)}, u32[]{:S(2)}) copy-start(s32[1,8]{1,0:T(1,128)} %param.31) | copy-start | bytes 100
  7.2 9.0 %copy-start.10 = (f32[128]{0:T(128)S(1)}, f32[128]{0:T(128)}, u32[]{:S(2)}) copy-start(f32[128]{0:T(128)} %param.25) | copy-start | bytes 1540
  19.8 9.1 %copy-start.9 = (s32[8,1,2,1]{0,3,2,1:T(1,128)S(1)}, s32[8,1,2,1]{0,3,2,1:T(1,128)}, u32[]{:S(2)}) copy-start(s32[8,1,2,1]{0,3,2,1:T(1,128)} %param.37) | copy-start | bytes 196
  19.8 74.6 %all-to-all-start = ((bf16[32,320,256]{2,1,0:T(8,128)(2,1)}), bf16[32,320,256]{2,1,0:T(8,128)(2,1)}, u32[]{:S(2)}, u32[]{:S(2)}) async-start(bf16[32,320,256]{2,1,0:T(8,128)(2,1)} %broadcast_in_dim.177), calls=%async_computation | async-start | bytes 10485760 | tf_op jit(solution)/shard_map/all_to_all | solution.py:199
  28.8 141.4 %reduce-scatter.2.cloned.1.call-start = ((), (), s32[]{:S(2)}) async-start(), calls=%async_computation.5 | async-start | bytes 1572864 | tf_op jit(solution)/shard_map/reduce_scatter | solution.py:275
  31.1 11.7 %copy-start.3 = (s32[10240]{0:T(1024)}, s32[10240]{0:T(1024)S(1)}, u32[]{:S(2)}) copy-start(s32[10240]{0:T(1024)S(1)} %get-tuple-element.46) | copy-start | bytes 122884
  31.1 11.7 %copy-start.4 = (s32[10240]{0:T(1024)}, s32[10240]{0:T(1024)S(1)}, u32[]{:S(2)}) copy-start(s32[10240]{0:T(1024)S(1)} %get-tuple-element.47) | copy-start | bytes 122884
  36.3 6.5 %copy-start.12 = (f32[2048]{0:T(1024)S(1)}, f32[2048]{0:T(1024)}, u32[]{:S(2)}) copy-start(f32[2048]{0:T(1024)} %param.20) | copy-start | bytes 24580
  42.9 4.2 copy-start.11
  133.4 30.1 %copy-start.7 = (s32[1,128,8]{1,2,0:T(8,128)S(1)}, s32[1,128,8]{1,2,0:T(8,128)}, u32[]{:S(2)}) copy-start(s32[1,128,8]{1,2,0:T(8,128)} %param.32) | copy-start | bytes 12292
  133.4 38.2 %copy-start.5 = (f32[2048]{0:T(1024)S(1)}, f32[2048]{0:T(1024)}, u32[]{:S(2)}) copy-start(f32[2048]{0:T(1024)} %param.27) | copy-start | bytes 24580
  133.5 58.6 %all-to-all-start.1 = ((bf16[1,32,144,256]{3,2,0,1:T(8,128)(2,1)}), bf16[1,32,144,256]{3,2,0,1:T(8,128)(2,1)}, u32[]{:S(2)}, u32[]{:S(2)}) async-start(bf16[1,32,144,256]{3,2,0,1:T(8,128)(2,1)} %bitcast.166), calls=%async_computation.2 | async-start | bytes 4718592 | tf_op jit(solution)/shard_map/all_to_all | solution.py:239
  171.7 1.9 copy-start.1
  325.3 6.4 %copy-start.6 = (f32[1,128,8]{1,2,0:T(8,128)S(1)}, f32[1,128,8]{1,2,0:T(8,128)}, u32[]{:S(2)}) copy-start(f32[1,128,8]{1,2,0:T(8,128)} %param.33) | copy-start | bytes 12292
  325.3 84.3 %all-to-all-start.3 = ((bf16[128,192,128]{2,1,0:T(8,128)(2,1)}), bf16[128,192,128]{2,1,0:T(8,128)(2,1)}, u32[]{:S(2)}, u32[]{:S(2)}) async-start(bf16[128,192,128]{2,1,0:T(8,128)(2,1)} %reshape_transpose_reshape.4), calls=%async_computation.4 | async-start | bytes 12582912 | tf_op jit(solution)/shard_map/all_to_all | solution.py:328
  420.8 3.5 copy-start.2
Sparse Core Ops, SparseCore 0:
  133.6 35.3 reduce-scatter.1
